TPU v7x, 256 devices: a whole 4x4x8 slice. The times are simulated.
256 devices in a mesh: dp: 16 (over y, x_lo, core), ctx: 8 (over z), tp: 2 (over x_hi).
Axes of the slice: x: 4 (x_hi: 2, x_lo: 2; x = x_hi * 2 + x_lo), y: 4, z: 8, core: 2. Of those that a mesh axis runs over, the one named last changes fastest.
Arguments:
- tokens: bfloat16 [16, 2048, 8192], P('dp', 'ctx', 'tp'), may hold values from -6 to 6
- queries: bfloat16 [16, 2048, 8192], P('dp', 'ctx', 'tp'), may hold values from -180 to 180
- k_weight: bfloat16 [8192, 512], P('dp', 'tp'), may hold values from -0.0625 to 0.0625
- v_weight: bfloat16 [8192, 512], P('dp', 'tp'), may hold values from -0.0625 to 0.0625
- doc_blocks: int32 [16, 16], P('dp', 'ctx'), may hold values from 0 to 3, never falling along the last dimension, each value on 1 to 8 neighbouring positions
Outputs:
- context: bfloat16 [16, 2048, 8192], P('dp', 'ctx', 'tp')
Inputs may be any that keep to these rules, and one draw needn't show every extreme that they name: `doc_blocks`: along each sequence the document numbers never fall; each document covers 1 to 8 whole blocks, one exactly 8.
All inputs are finite; a program needn't handle non-finite values.
Results may differ from a plain program's by a relative error of at most 0.012.
The roundings to bfloat16 on the way count: a program that leaves them out, or rounds other values in their place, can miss the bound.
Values may be sent and summed in bfloat16 or wider, within the bound.
No kernel may reach another device: no remote copies, remote signals or barrier semaphores. Data moves between devices by JAX's collectives and lax.ppermute only.
A program may use at most 192 MiB of HBM per device.

v0:
```python
import math

import jax
import jax.numpy as jnp
from jax import lax
from jax.experimental import pallas as pl
from jax.experimental.pallas import tpu as pltpu
from jax.sharding import PartitionSpec as P


HD = 128
BLOCK = 128
LOOKBACK = 7


ROPE_BASE = 500000.0
YARN_FACTOR = 16.0
PRETRAIN_CONTEXT = 8192.0
BETA_FAST = 32.0
BETA_SLOW = 1.0
ATTN_FACTOR = (1.0 + 0.1 * math.log(16.0)) ** 2
MASKED_SCORE = -1e30


def yarn_tables(positions):
    counter = jnp.arange(HD // 2, dtype=jnp.float32)
    base_freq = ROPE_BASE ** (-2.0 * counter / HD)
    wave_ratio = PRETRAIN_CONTEXT * base_freq / (2.0 * math.pi)
    ramp_value = jnp.clip((wave_ratio - BETA_SLOW) / (BETA_FAST - BETA_SLOW), 0.0, 1.0)
    frequency = ramp_value * base_freq + (1.0 - ramp_value) * base_freq / YARN_FACTOR
    angles = positions.astype(jnp.float32)[:, None] * frequency[None, :]
    cosine = jnp.cos(angles)
    sine_table = jnp.sin(angles)
    return (
        jnp.concatenate([cosine, cosine], axis=-1),
        jnp.concatenate([sine_table, sine_table], axis=-1),
    )


def rotate(vectors, cosine, sine_table):
    half_width = vectors.shape[-1] // 2
    lower_half = vectors[..., :half_width]
    upper_half = vectors[..., half_width:]
    turned = jnp.concatenate([-upper_half, lower_half], axis=-1)
    return vectors * cosine[:, None, :] + turned * sine_table[:, None, :]


def dense_kernel(vis_ref, q_ref, k_ref, v_ref, o_ref, qs_ref):
    rows = o_ref.shape[0]
    group = o_ref.shape[1] // HD
    for g in range(group):
        qs_ref[g * rows:(g + 1) * rows, :] = q_ref[:, g * HD:(g + 1) * HD]
    visible = vis_ref[...] != 0
    keys = k_ref[...]
    values = v_ref[...]
    height = keys.shape[0]
    part = group // 2
    for half in range(2):
        stacked = qs_ref[half * part * rows:(half + 1) * part * rows, :]
        scores = lax.dot_general(
            stacked, keys, (((1,), (1,)), ((), ())), preferred_element_type=jnp.float32
        )
        scores = jnp.where(visible[None], scores.reshape(part, rows, height), MASKED_SCORE)
        row_max = jnp.max(scores, axis=2, keepdims=True)
        probs = jnp.where(visible[None], jnp.exp(scores - row_max), 0.0)
        row_sum = jnp.sum(probs, axis=2, keepdims=True)
        mixed = jnp.dot(
            probs.reshape(part * rows, height).astype(jnp.bfloat16),
            values,
            preferred_element_type=jnp.float32,
        )
        result = mixed.reshape(part, rows, HD) / row_sum
        for g in range(part):
            head = half * part + g
            o_ref[:, head * HD:(head + 1) * HD] = result[g].astype(o_ref.dtype)


def dense_attention(visible, query_rot, kv_all, kv_heads, head):
    row_count, width = query_rot.shape
    height = kv_all.shape[0]
    q_blocks = row_count // BLOCK
    group_width = width // kv_heads
    group = group_width // HD
    return pl.pallas_call(
        dense_kernel,
        grid=(q_blocks,),
        in_specs=[
            pl.BlockSpec((BLOCK, height), lambda qb: (qb, 0)),
            pl.BlockSpec((BLOCK, group_width), lambda qb: (qb, head)),
            pl.BlockSpec((height, HD), lambda qb: (0, 0)),
            pl.BlockSpec((height, HD), lambda qb: (0, 1)),
        ],
        out_specs=pl.BlockSpec((BLOCK, group_width), lambda qb: (qb, 0)),
        scratch_shapes=[pltpu.VMEM((group * BLOCK, HD), jnp.bfloat16)],
        out_shape=jax.ShapeDtypeStruct((row_count, group_width), jnp.bfloat16),
        compiler_params=pltpu.CompilerParams(vmem_limit_bytes=48 * 1024 * 1024),
        cost_estimate=pl.CostEstimate(
            flops=4 * row_count * group_width * height,
            transcendentals=row_count * group * height,
            bytes_accessed=4 * row_count * group_width + 2 * kv_all.size + 4 * row_count * height,
        ),
    )(visible, query_rot, kv_all, kv_all)


def shift_pairs(count, step):
    return [(i, i + step) for i in range(count - step)]


def make_body(n_ctx):
    def body(tokens, queries, k_weight, v_weight, doc_blocks):
        return layer(tokens, queries, k_weight, v_weight, doc_blocks)

    def layer(tokens, queries, k_weight, v_weight, doc_blocks):
        local_tokens = tokens[0]
        row_count, feat_half = local_tokens.shape
        ctx_rank = lax.axis_index("ctx")
        tp_rank = lax.axis_index("tp")
        kv_width = k_weight.shape[1]
        kv_heads = kv_width // HD

        positions = ctx_rank * row_count + jnp.arange(row_count, dtype=jnp.int32)
        cosine, sine_table = yarn_tables(positions)
        local_queries = queries[0]
        query_heads = local_queries.shape[1] // HD
        query_rot = (
            (
                rotate(
                    local_queries.astype(jnp.float32).reshape(row_count, query_heads, HD),
                    cosine,
                    sine_table,
                )
                * (ATTN_FACTOR / math.sqrt(HD))
            )
            .reshape(row_count, query_heads * HD)
            .astype(jnp.bfloat16)
        )
        partner_tokens = lax.ppermute(local_tokens, "tp", [(0, 1), (1, 0)])
        local_docs = doc_blocks[0]
        blocks_here = row_count // BLOCK

        outputs = []
        visible = None
        earlier_rows = None
        for head in range(kv_heads):
            cols = slice(head * HD, (head + 1) * HD)
            joined = jnp.concatenate([k_weight[:, cols], v_weight[:, cols]], axis=1)
            weights = lax.all_gather(joined, "dp", axis=0, tiled=True)
            weights = weights.reshape(2, feat_half, 2 * HD)
            proj = jnp.dot(local_tokens, weights[tp_rank], preferred_element_type=jnp.float32)
            proj = proj + jnp.dot(
                partner_tokens, weights[1 - tp_rank], preferred_element_type=jnp.float32
            )
            if earlier_rows is not None:
                proj = proj + 0.0 * earlier_rows[:1, :1].astype(jnp.float32)
            key_rows = (
                rotate(proj[:, :HD].reshape(row_count, 1, HD), cosine, sine_table)
                .reshape(row_count, HD)
                .astype(jnp.bfloat16)
            )
            value_rows = proj[:, HD:].astype(jnp.bfloat16)
            kv_rows = jnp.concatenate([key_rows, value_rows], axis=1)
            earlier_rows = kv_rows

            with_docs = visible is None
            doc_rows = jnp.zeros((16, 2 * HD), jnp.bfloat16)
            window_kv = []
            window_docs = []
            need = LOOKBACK
            step = 1
            while need > 0:
                take = min(need, blocks_here)
                pairs = shift_pairs(n_ctx, step)
                payload = kv_rows[(blocks_here - take) * BLOCK:]
                if with_docs:
                    tagged = doc_rows.at[0, :take].set(
                        local_docs[blocks_here - take:].astype(jnp.bfloat16)
                    )
                    payload = jnp.concatenate([payload, tagged], axis=0)
                arrived = lax.ppermute(payload, "ctx", pairs)
                window_kv.insert(0, arrived[:take * BLOCK])
                if with_docs:
                    window_docs.insert(0, arrived[take * BLOCK, :take].astype(jnp.int32))
                need -= take
                step += 1
            window_kv.append(kv_rows)
            kv_all = jnp.concatenate(window_kv, axis=0)
            height = kv_all.shape[0]
            if with_docs:
                window_docs.append(local_docs)
                block_docs = jnp.concatenate(window_docs, axis=0)
                key_pos = (
                    ctx_rank * row_count - (height - row_count) + jnp.arange(height, dtype=jnp.int32)
                )
                key_docs = jnp.repeat(block_docs, BLOCK)
                query_docs = jnp.repeat(local_docs, BLOCK)
                visible = (
                    (key_pos[None, :] <= positions[:, None])
                    & (key_pos[None, :] >= 0)
                    & (key_docs[None, :] == query_docs[:, None])
                ).astype(jnp.int32)
            outputs.append(dense_attention(visible, query_rot, kv_all, kv_heads, head))
        context = jnp.concatenate(outputs, axis=1)
        return context[None]

    return body


def solution(mesh):
    placed = (
        P("dp", "ctx", "tp"),
        P("dp", "ctx", "tp"),
        P("dp", "tp"),
        P("dp", "tp"),
        P("dp", "ctx"),
    )
    return jax.shard_map(
        make_body(mesh.shape["ctx"]),
        mesh=mesh,
        in_specs=placed,
        out_specs=P("dp", "ctx", "tp"),
        check_vma=False,
    )
```

profile of v0, /device:TPU:100, one launch (start us, length us, event | category | flops | bytes accessed | tf_op | source)
XLA Modules:
  0.0 193.0 jit_solution(7752295948777992120)
XLA Ops:
  11.1 2.1 %convert_bitcast_fusion = f32[32,8,32,128]{3,1,2,0:T(8,128)S(1)} fusion(bf16[1,256,4096]{2,1,0:T(8,128)(2,1)} %param.14), kind=kLoop, calls=%fused_computation | loop fusion | flops 1048576 | bytes 6291456
  13.2 2.7 %copy.15 = f32[32,8,32,128]{3,2,1,0:T(8,128)} copy(f32[32,8,32,128]{3,1,2,0:T(8,128)S(1)} %convert_bitcast_fusion) | data formatting | bytes 8388608
  18.3 7.9 %slice_negate_fusion = (f32[256,32,64]{2,1,0:T(8,128)}, f32[256,32,64]{2,1,0:T(8,128)}) fusion(f32[256,32,128]{2,1,0:T(8,128)} %bitcast.92), kind=kLoop, calls=%fused_computation.6 | loop fusion | flops 524288 | bytes 8388608 | tf_op jit(solution)/shard_map/neg | solution.py:44
  26.2 39.2 %all-gather.3.cloned.1.call-done = bf16[8192,256]{1,0:T(8,128)(2,1)} async-done(((bf16[512,256]{1,0:T(8,128)(2,1)}), bf16[8192,256]{1,0:T(8,128)(2,1)}) %all-gather.3.cloned.1.call-update) | async-done | bytes 4194320 | tf_op jit(solution)/shard_map/all_gather | solution.py:147
  65.3 3.1 %fusion.10 = f32[256,256]{0,1:T(8,128)S(1)} fusion(bf16[2,4096,256]{2,1,0:T(8,128)(2,1)} %bitcast.98, s32[]{:T(128)S(6)} %select_n.8, bf16[1,256,4096]{2,1,0:T(8,128)(2,1)} %param.13), kind=kOutput, calls=%fused_computation.15 | convolution fusion | flops 536870912 | bytes 4456452 | tf_op jit(solution)/shard_map/dot_general | solution.py:149
  68.4 9.7 %collective-permute-done = bf16[256,4096]{1,0:T(8,128)(2,1)S(1)} collective-permute-done((bf16[256,4096]{1,0:T(8,128)(2,1)}, bf16[256,4096]{1,0:T(8,128)(2,1)S(1)}, u32[]{:S(2)}, u32[]{:S(2)}) %collective-permute-start) | collective-permute-done | bytes 2097184 | tf_op jit(solution)/shard_map/ppermute | solution.py:137
  79.2 5.9 %collective-permute-start.2 = (bf16[272,256]{1,0:T(8,128)(2,1)S(1)}, bf16[272,256]{1,0:T(8,128)(2,1)}, u32[]{:S(2)}, u32[]{:S(2)}) collective-permute-start(bf16[272,256]{1,0:T(8,128)(2,1)S(1)} %fusion.33), channel_id=1, source_target_pairs={{0,6},{2,8},{4,10},{6,12},{8,14},{1,7},{3,9},{5,11},{7,13},{9,15},... | collective-permute-start | bytes 417800 | tf_op jit(solution)/shard_map/ppermute | solution.py:179
  85.1 1.9 collective-permute-start.3
  87.1 2.9 %collective-permute-start.4 = (bf16[272,256]{1,0:T(8,128)(2,1)S(1)}, bf16[272,256]{1,0:T(8,128)(2,1)}, u32[]{:S(2)}, u32[]{:S(2)}) collective-permute-start(bf16[272,256]{1,0:T(8,128)(2,1)S(1)} %fusion.33), channel_id=1, source_target_pairs={{0,2},{2,4},{4,6},{6,8},{8,10},{10,12},{12,14},{1,3},{3,5},{5,7},{... | collective-permute-start | bytes 417800 | tf_op jit(solution)/shard_map/ppermute | solution.py:179
  90.5 17.2 %all-gather.5.cloned.1.call-done = bf16[8192,256]{1,0:T(8,128)(2,1)} async-done(((bf16[512,256]{1,0:T(8,128)(2,1)}), bf16[8192,256]{1,0:T(8,128)(2,1)}) %all-gather.5.cloned.1.call-update) | async-done | bytes 4194320 | tf_op jit(solution)/shard_map/all_gather | solution.py:147
  107.7 3.1 %fusion.6 = f32[256,256]{0,1:T(8,128)S(1)} fusion(bf16[2,4096,256]{2,1,0:T(8,128)(2,1)} %bitcast.96, s32[]{:T(128)S(6)} %select_n.8, bf16[1,256,4096]{2,1,0:T(8,128)(2,1)} %param.13), kind=kOutput, calls=%fused_computation.11 | convolution fusion | flops 536870912 | bytes 4456452 | tf_op jit(solution)/shard_map/dot_general | solution.py:149
  111.6 2.4 %fusion.28 = f32[256,256]{1,0:T(8,128)S(1)} fusion(f32[256,256]{0,1:T(8,128)S(1)} %fusion.6, bf16[256,4096]{1,0:T(8,128)(2,1)S(1)} %collective-permute-done, bf16[2,4096,256]{2,1,0:T(8,128)(2,1)} %bitcast.97, s32[]{:T(128)S(6)} %select_n.9, f32[]{:T(128)} %bitcast.19), kind=kOutput, calls=%fused_computation.26 | convolution fusion | flops 537001984 | bytes 4719108 | tf_op jit(solution)/shard_map/dot_general | solution.py:150
  114.7 4.9 %collective-permute-start.1 = (bf16[144,256]{1,0:T(8,128)(2,1)S(1)}, bf16[144,256]{1,0:T(8,128)(2,1)S(1)}, u32[]{:S(2)}, u32[]{:S(2)}) collective-permute-start(bf16[144,256]{1,0:T(8,128)(2,1)S(1)} %fusion.41), channel_id=1, source_target_pairs={{0,8},{2,10},{4,12},{6,14},{1,9},{3,11},{5,13},{7,15},{16,24},{18,... | collective-permute-start | bytes 221192 | tf_op jit(solution)/shard_map/ppermute | solution.py:179
  119.9 1.5 collective-permute-start.5
  123.0 1.3 copy-done.2
  124.3 8.5 %fusion.3.q_ref = bf16[256,4096]{1,0:T(8,128)(2,1)S(1)} fusion(bf16[1,256,4096]{2,1,0:T(8,128)(2,1)S(1)} %copy-done.2, f32[32,8,32,128]{3,2,1,0:T(8,128)S(1)} %bitcast.93, f32[32,8,32,128]{3,2,1,0:T(8,128)S(1)} %bitcast.94), kind=kLoop, calls=%fused_computation.5 | loop fusion | flops 5242880 | bytes 12582912 | tf_op jit(solution)/shard_map/convert_element_type | solution.py:135
  132.9 1.9 collective-permute-start.6
  134.8 1.9 collective-permute-start.7
  137.9 5.1 %collective-permute-done.6 = bf16[256,256]{1,0:T(8,128)(2,1)S(1)} collective-permute-done((bf16[256,256]{1,0:T(8,128)(2,1)S(1)}, bf16[256,256]{1,0:T(8,128)(2,1)S(1)}, u32[]{:S(2)}, u32[]{:S(2)}) %collective-permute-start.6) | collective-permute-done | bytes 131104 | tf_op jit(solution)/shard_map/ppermute | solution.py:179
  143.0 8.3 %collective-permute-start.8 = (bf16[256,256]{1,0:T(8,128)(2,1)S(1)}, bf16[256,256]{1,0:T(8,128)(2,1)S(1)}, u32[]{:S(2)}, u32[]{:S(2)}) collective-permute-start(bf16[256,256]{1,0:T(8,128)(2,1)S(1)} %pad_maximum_fusion.3), channel_id=1, source_target_pairs={{0,2},{2,4},{4,6},{6,8},{8,10},{10,12},{12,14},{1,3},{3,5},{5,7},{... | collective-permute-start | bytes 393224 | tf_op jit(solution)/shard_map/ppermute | solution.py:179
  151.4 2.2 %collective-permute-done.8 = bf16[256,256]{1,0:T(8,128)(2,1)S(1)} collective-permute-done((bf16[256,256]{1,0:T(8,128)(2,1)S(1)}, bf16[256,256]{1,0:T(8,128)(2,1)S(1)}, u32[]{:S(2)}, u32[]{:S(2)}) %collective-permute-start.8) | collective-permute-done | bytes 131104 | tf_op jit(solution)/shard_map/ppermute | solution.py:179
  161.3 11.6 %shard_map.56 = bf16[256,2048]{1,0:T(8,128)(2,1)S(1)} custom-call(s32[256,1152]{1,0:T(8,128)S(1)} %and_convert_fusion.vis_ref, bf16[256,4096]{1,0:T(8,128)(2,1)S(1)} %fusion.3.q_ref, bf16[1152,256]{1,0:T(8,128)(2,1)S(1)} %constant_dynamic-update-slice_fusion.k_ref.v_ref, bf16[1152,256]{1,0:T(8,128)(2,1)S(1)} %constant_dynamic-update-slice_fusion.k_ref.v_ref), custom_call_target="tpu_custom_call" | custom-call | flops 2415919104 | bytes 3866624 | tf_op jit(solution)/shard_map/pallas_call | solution.py:84
  173.0 11.6 %shard_map.55 = bf16[256,2048]{1,0:T(8,128)(2,1)S(1)} custom-call(s32[256,1152]{1,0:T(8,128)S(1)} %and_convert_fusion.vis_ref, bf16[256,4096]{1,0:T(8,128)(2,1)S(1)} %fusion.3.q_ref, bf16[1152,256]{1,0:T(8,128)(2,1)S(1)} %fusion.34.k_ref.v_ref, bf16[1152,256]{1,0:T(8,128)(2,1)S(1)} %fusion.34.k_ref.v_ref), custom_call_target="tpu_custom_call" | custom-call | flops 2415919104 | bytes 3866624 | tf_op jit(solution)/shard_map/pallas_call | solution.py:84
  184.6 1.5 maximum_bitcast_fusion
  (66 shorter events, 19.2 us)
Async XLA Ops:
  6.5 58.8 %all-gather.3.cloned.1.call-start = ((), (), s32[]{:S(2)}) async-start(), calls=%async_computation | async-start | bytes 4456448 | tf_op jit(solution)/shard_map/all_gather | solution.py:147
  8.4 99.3 %all-gather.5.cloned.1.call-start = ((), (), s32[]{:S(2)}) async-start(), calls=%async_computation.1 | async-start | bytes 4456448 | tf_op jit(solution)/shard_map/all_gather | solution.py:147
  9.2 68.8 %collective-permute-start = (bf16[256,4096]{1,0:T(8,128)(2,1)}, bf16[256,4096]{1,0:T(8,128)(2,1)S(1)}, u32[]{:S(2)}, u32[]{:S(2)}) collective-permute-start(bf16[256,4096]{1,0:T(8,128)(2,1)} %bitcast.95), channel_id=1, source_target_pairs={{0,1},{1,0},{2,3},{3,2},{4,5},{5,4},{6,7},{7,6},{8,9},{9,8},{10,11... | collective-permute-start | bytes 6291464 | tf_op jit(solution)/shard_map/ppermute | solution.py:137
  13.2 3.9 %copy-start.4 = (s32[1,2]{1,0:T(1,128)S(1)}, s32[1,2]{1,0:T(1,128)}, u32[]{:S(2)}) copy-start(s32[1,2]{1,0:T(1,128)} %param.17) | copy-start | bytes 28
  65.3 12.8 %copy-start.3 = (bf16[8192,256]{1,0:T(8,128)(2,1)S(1)}, bf16[8192,256]{1,0:T(8,128)(2,1)}, u32[]{:S(2)}) copy-start(bf16[8192,256]{1,0:T(8,128)(2,1)} %all-gather.3.cloned.1.call-done) | copy-start | bytes 12582916
  79.2 74.5 %collective-permute-start.2 = (bf16[272,256]{1,0:T(8,128)(2,1)S(1)}, bf16[272,256]{1,0:T(8,128)(2,1)}, u32[]{:S(2)}, u32[]{:S(2)}) collective-permute-start(bf16[272,256]{1,0:T(8,128)(2,1)S(1)} %fusion.33), channel_id=1, source_target_pairs={{0,6},{2,8},{4,10},{6,12},{8,14},{1,7},{3,9},{5,11},{7,13},{9,15},... | collective-permute-start | bytes 417800 | tf_op jit(solution)/shard_map/ppermute | solution.py:179
  85.1 69.7 %collective-permute-start.3 = (bf16[272,256]{1,0:T(8,128)(2,1)S(1)}, bf16[272,256]{1,0:T(8,128)(2,1)}, u32[]{:S(2)}, u32[]{:S(2)}) collective-permute-start(bf16[272,256]{1,0:T(8,128)(2,1)S(1)} %fusion.33), channel_id=1, source_target_pairs={{0,4},{2,6},{4,8},{6,10},{8,12},{10,14},{1,5},{3,7},{5,9},{7,11},{... | collective-permute-start | bytes 417800 | tf_op jit(solution)/shard_map/ppermute | solution.py:179
  87.1 69.0 %collective-permute-start.4 = (bf16[272,256]{1,0:T(8,128)(2,1)S(1)}, bf16[272,256]{1,0:T(8,128)(2,1)}, u32[]{:S(2)}, u32[]{:S(2)}) collective-permute-start(bf16[272,256]{1,0:T(8,128)(2,1)S(1)} %fusion.33), channel_id=1, source_target_pairs={{0,2},{2,4},{4,6},{6,8},{8,10},{10,12},{12,14},{1,3},{3,5},{5,7},{... | collective-permute-start | bytes 417800 | tf_op jit(solution)/shard_map/ppermute | solution.py:179
  107.7 13.7 %copy-start.1 = (f32[256,32,64]{2,1,0:T(8,128)S(1)}, f32[256,32,64]{2,1,0:T(8,128)}, u32[]{:S(2)}) copy-start(f32[256,32,64]{2,1,0:T(8,128)} %get-tuple-element.46) | copy-start | bytes 6291460
  110.8 10.6 %copy-start = (f32[256,32,64]{2,1,0:T(8,128)S(1)}, f32[256,32,64]{2,1,0:T(8,128)}, u32[]{:S(2)}) copy-start(f32[256,32,64]{2,1,0:T(8,128)} %get-tuple-element.45) | copy-start | bytes 6291460
  114.7 20.1 %collective-permute-start.1 = (bf16[144,256]{1,0:T(8,128)(2,1)S(1)}, bf16[144,256]{1,0:T(8,128)(2,1)S(1)}, u32[]{:S(2)}, u32[]{:S(2)}) collective-permute-start(bf16[144,256]{1,0:T(8,128)(2,1)S(1)} %fusion.41), channel_id=1, source_target_pairs={{0,8},{2,10},{4,12},{6,14},{1,9},{3,11},{5,13},{7,15},{16,24},{18,... | collective-permute-start | bytes 221192 | tf_op jit(solution)/shard_map/ppermute | solution.py:179
  119.9 12.9 %collective-permute-start.5 = (bf16[128,256]{1,0:T(8,128)(2,1)S(1)}, bf16[128,256]{1,0:T(8,128)(2,1)S(1)}, u32[]{:S(2)}, u32[]{:S(2)}) collective-permute-start(bf16[128,256]{1,0:T(8,128)(2,1)S(1)} %fusion.42), channel_id=1, source_target_pairs={{0,8},{2,10},{4,12},{6,14},{1,9},{3,11},{5,13},{7,15},{16,24},{18,... | collective-permute-start | bytes 196616 | tf_op jit(solution)/shard_map/ppermute | solution.py:179
  122.7 1.6 copy-start.2
  132.9 10.1 %collective-permute-start.6 = (bf16[256,256]{1,0:T(8,128)(2,1)S(1)}, bf16[256,256]{1,0:T(8,128)(2,1)S(1)}, u32[]{:S(2)}, u32[]{:S(2)}) collective-permute-start(bf16[256,256]{1,0:T(8,128)(2,1)S(1)} %pad_maximum_fusion.3), channel_id=1, source_target_pairs={{0,6},{2,8},{4,10},{6,12},{8,14},{1,7},{3,9},{5,11},{7,13},{9,15},... | collective-permute-start | bytes 393224 | tf_op jit(solution)/shard_map/ppermute | solution.py:179
  134.8 16.5 %collective-permute-start.7 = (bf16[256,256]{1,0:T(8,128)(2,1)S(1)}, bf16[256,256]{1,0:T(8,128)(2,1)S(1)}, u32[]{:S(2)}, u32[]{:S(2)}) collective-permute-start(bf16[256,256]{1,0:T(8,128)(2,1)S(1)} %pad_maximum_fusion.3), channel_id=1, source_target_pairs={{0,4},{2,6},{4,8},{6,10},{8,12},{10,14},{1,5},{3,7},{5,9},{7,11},{... | collective-permute-start | bytes 393224 | tf_op jit(solution)/shard_map/ppermute | solution.py:179
  143.0 10.6 %collective-permute-start.8 = (bf16[256,256]{1,0:T(8,128)(2,1)S(1)}, bf16[256,256]{1,0:T(8,128)(2,1)S(1)}, u32[]{:S(2)}, u32[]{:S(2)}) collective-permute-start(bf16[256,256]{1,0:T(8,128)(2,1)S(1)} %pad_maximum_fusion.3), channel_id=1, source_target_pairs={{0,2},{2,4},{4,6},{6,8},{8,10},{10,12},{12,14},{1,3},{3,5},{5,7},{... | collective-permute-start | bytes 393224 | tf_op jit(solution)/shard_map/ppermute | solution.py:179
Sparse Core Ops, SparseCore 0:
  9.2 56.0 all-gather.2
  67.2 40.5 all-gather.4
where the time goes:
time: 194 us; the launch traced here: 193 us
  waiting for transfers between devices  73.4 us (38%)
  other arithmetic  30.5 us (16%)
  starting transfers between devices  30 us (15%)
  Pallas kernels  23.3 us (12%)
  between operations  15.2 us (8%)
  local copies, waits for them, and re-layouts  11.3 us (6%)
  matrix products  9.3 us (5%)
    all_gather x2, waiting for transfers between devices, layer(): weights = lax.all_gather(joined, 'dp', axis=0, tiled=True)  56.4 us
    ppermute x8, starting transfers between devices, layer(): arrived = lax.ppermute(payload, 'ctx', pairs)  29.3 us
    pallas_call x2, Pallas kernels, dense_attention(): pl.pallas_call(dense_kernel, grid=(q_blocks,), in_specs=[pl.BlockSpec((BL...  23.3 us
    ppermute x1, waiting for transfers between devices, layer(): partner_tokens = lax.ppermute(local_tokens, 'tp', [(0, 1), (1, 0)])  9.69 us
    convert_element_type x1, other arithmetic, layer(): query_rot = (rotate(local_queries.astype(jnp.float32).reshape(row_count,...  8.51 us
    neg x1, other arithmetic, rotate(): turned = jnp.concatenate([-upper_half, lower_half], axis=-1)  7.88 us
    ppermute x8, waiting for transfers between devices, layer(): arrived = lax.ppermute(payload, 'ctx', pairs)  7.3 us
    unnamed x19, local copies, waits for them, and re-layouts  6.79 us
  transfers between devices with their start and end apart: 11, of which 5 were waited for; matrix products, arithmetic and copies ran while one was open for 21% of the time, Pallas kernels for 0%

commit v1 on v0

--- a/solution.py
+++ b/solution.py
@@ -45,11 +45,16 @@
     return vectors * cosine[:, None, :] + turned * sine_table[:, None, :]
 
 
-def dense_kernel(vis_ref, q_ref, k_ref, v_ref, o_ref, qs_ref):
+def dense_kernel(vis_ref, cos_ref, sin_ref, q_ref, k_ref, v_ref, o_ref, qs_ref):
     rows = o_ref.shape[0]
     group = o_ref.shape[1] // HD
+    cosine = cos_ref[...]
+    signed_sine = sin_ref[...]
     for g in range(group):
-        qs_ref[g * rows:(g + 1) * rows, :] = q_ref[:, g * HD:(g + 1) * HD]
+        raw = q_ref[:, g * HD:(g + 1) * HD].astype(jnp.float32)
+        turned = pltpu.roll(raw, HD // 2, 1) * signed_sine
+        rotated = (raw * cosine + turned) * (ATTN_FACTOR / math.sqrt(HD))
+        qs_ref[g * rows:(g + 1) * rows, :] = rotated.astype(jnp.bfloat16)
     visible = vis_ref[...] != 0
     keys = k_ref[...]
     values = v_ref[...]
@@ -75,7 +80,7 @@
             o_ref[:, head * HD:(head + 1) * HD] = result[g].astype(o_ref.dtype)
 
 
-def dense_attention(visible, query_rot, kv_all, kv_heads, head):
+def dense_attention(visible, cosine, signed_sine, query_rot, kv_all, kv_heads, head):
     row_count, width = query_rot.shape
     height = kv_all.shape[0]
     q_blocks = row_count // BLOCK
@@ -86,6 +91,8 @@
         grid=(q_blocks,),
         in_specs=[
             pl.BlockSpec((BLOCK, height), lambda qb: (qb, 0)),
+            pl.BlockSpec((BLOCK, HD), lambda qb: (qb, 0)),
+            pl.BlockSpec((BLOCK, HD), lambda qb: (qb, 0)),
             pl.BlockSpec((BLOCK, group_width), lambda qb: (qb, head)),
             pl.BlockSpec((height, HD), lambda qb: (0, 0)),
             pl.BlockSpec((height, HD), lambda qb: (0, 1)),
@@ -99,7 +106,7 @@
             transcendentals=row_count * group * height,
             bytes_accessed=4 * row_count * group_width + 2 * kv_all.size + 4 * row_count * height,
         ),
-    )(visible, query_rot, kv_all, kv_all)
+    )(visible, cosine, signed_sine, query_rot, kv_all, kv_all)
 
 
 def shift_pairs(count, step):
@@ -120,20 +127,11 @@
 
         positions = ctx_rank * row_count + jnp.arange(row_count, dtype=jnp.int32)
         cosine, sine_table = yarn_tables(positions)
-        local_queries = queries[0]
-        query_heads = local_queries.shape[1] // HD
-        query_rot = (
-            (
-                rotate(
-                    local_queries.astype(jnp.float32).reshape(row_count, query_heads, HD),
-                    cosine,
-                    sine_table,
-                )
-                * (ATTN_FACTOR / math.sqrt(HD))
-            )
-            .reshape(row_count, query_heads * HD)
-            .astype(jnp.bfloat16)
+        query_rot = queries[0]
+        half_sign = jnp.concatenate(
+            [-jnp.ones((HD // 2,), jnp.float32), jnp.ones((HD // 2,), jnp.float32)]
         )
+        signed_sine = sine_table * half_sign[None, :]
         partner_tokens = lax.ppermute(local_tokens, "tp", [(0, 1), (1, 0)])
         local_docs = doc_blocks[0]
         blocks_here = row_count // BLOCK
@@ -198,7 +196,11 @@
                     & (key_pos[None, :] >= 0)
                     & (key_docs[None, :] == query_docs[:, None])
                 ).astype(jnp.int32)
-            outputs.append(dense_attention(visible, query_rot, kv_all, kv_heads, head))
+            outputs.append(
+                dense_attention(
+                    visible, cosine, signed_sine, query_rot, kv_all, kv_heads, head
+                )
+            )
         context = jnp.concatenate(outputs, axis=1)
         return context[None]
 

time: 194 us -> 192 us (0.990)
  other arithmetic: 30.5 us -> 10.7 us
  waiting for transfers between devices: 73.4 us -> 92.8 us
  local copies, waits for them, and re-layouts: 11.3 us -> 7.16 us
  starting transfers between devices: 30 us -> 32.6 us
    all_gather x2, waiting for transfers between devices: 56.4 us -> 69.5 us  [layer(): weights = lax.all_gather(joined, 'dp', axis=0, tiled=True)]
    convert_element_type x1 -> x0, other arithmetic: 8.51 us -> none  [layer(): query_rot = (rotate(local_queries.astype(jnp.float32).reshape(row_count,...]
    neg x1 -> x0, other arithmetic: 7.88 us -> none  [rotate(): turned = jnp.concatenate([-upper_half, lower_half], axis=-1)]
    ppermute x8, waiting for transfers between devices: 7.3 us -> 13.5 us  [layer(): arrived = lax.ppermute(payload, 'ctx', pairs)]
    unnamed x19 -> x26, local copies, waits for them, and re-layouts: 6.79 us -> 2.83 us
    ppermute x8, starting transfers between devices: 29.3 us -> 32 us  [layer(): arrived = lax.ppermute(payload, 'ctx', pairs)]
    unnamed x1 -> x0, other arithmetic: 2.07 us -> none
  transfers between devices with their start and end apart: 11 -> 11, of which waited for: 5 -> 7; matrix products, arithmetic and copies ran while one was open for 21% -> 8% of each run, Pallas kernels for 0% -> 0%
where the time goes in v1:
time: 192 us; the launch traced here: 189 us
  waiting for transfers between devices  92.8 us (48%)
  starting transfers between devices  32.6 us (17%)
  Pallas kernels  23.4 us (12%)
  between operations  15.1 us (8%)
  other arithmetic  10.7 us (6%)
  matrix products  7.64 us (4%)
  local copies, waits for them, and re-layouts  7.16 us (4%)
    all_gather x2, waiting for transfers between devices, layer(): weights = lax.all_gather(joined, 'dp', axis=0, tiled=True)  69.5 us
    ppermute x8, starting transfers between devices, layer(): arrived = lax.ppermute(payload, 'ctx', pairs)  32 us
    pallas_call x2, Pallas kernels, dense_attention(): pl.pallas_call(dense_kernel, grid=(q_blocks,), in_specs=[pl.BlockSpec((BL...  23.4 us
    ppermute x8, waiting for transfers between devices, layer(): arrived = lax.ppermute(payload, 'ctx', pairs)  13.5 us
    ppermute x1, waiting for transfers between devices, layer(): partner_tokens = lax.ppermute(local_tokens, 'tp', [(0, 1), (1, 0)])  9.72 us
    dot_general x2, matrix products, layer(): jnp.dot(local_tokens, weights[tp_rank], preferred_element_type=jnp.float32)  6.15 us
  transfers between devices with their start and end apart: 11, of which 7 were waited for; matrix products, arithmetic and copies ran while one was open for 8% of the time, Pallas kernels for 0%

profile of v1, /device:TPU:100, one launch (start us, length us, event | category | flops | bytes accessed | tf_op | source)
XLA Modules:
  0.0 189.4 jit_solution(9307212530821697510)
XLA Ops:
  6.5 1.1 fusion.51
  12.2 53.1 %all-gather.3.cloned.1.call-done = bf16[8192,256]{1,0:T(8,128)(2,1)} async-done(((bf16[512,256]{1,0:T(8,128)(2,1)}), bf16[8192,256]{1,0:T(8,128)(2,1)}) %all-gather.3.cloned.1.call-update) | async-done | bytes 4194320 | tf_op jit(solution)/shard_map/all_gather | solution.py:145
  65.3 3.1 %fusion.6 = f32[256,256]{0,1:T(8,128)S(1)} fusion(bf16[2,4096,256]{2,1,0:T(8,128)(2,1)} %bitcast.78, s32[]{:T(128)S(6)} %select_n.8, bf16[1,256,4096]{2,1,0:T(8,128)(2,1)} %param.13), kind=kOutput, calls=%fused_computation.7 | convolution fusion | flops 536870912 | bytes 4456452 | tf_op jit(solution)/shard_map/dot_general | solution.py:147
  68.4 9.7 %collective-permute-done = bf16[256,4096]{1,0:T(8,128)(2,1)S(1)} collective-permute-done((bf16[256,4096]{1,0:T(8,128)(2,1)}, bf16[256,4096]{1,0:T(8,128)(2,1)S(1)}, u32[]{:S(2)}, u32[]{:S(2)}) %collective-permute-start) | collective-permute-done | bytes 2097184 | tf_op jit(solution)/shard_map/ppermute | solution.py:135
  79.9 5.9 %collective-permute-start.2 = (bf16[272,256]{1,0:T(8,128)(2,1)}, bf16[272,256]{1,0:T(8,128)(2,1)}, u32[]{:S(2)}, u32[]{:S(2)}) collective-permute-start(bf16[272,256]{1,0:T(8,128)(2,1)} %fusion.29), channel_id=1, source_target_pairs={{0,6},{2,8},{4,10},{6,12},{8,14},{1,7},{3,9},{5,11},{7,13},{9,15},... | collective-permute-start | bytes 417800 | tf_op jit(solution)/shard_map/ppermute | solution.py:177
  85.8 1.9 %collective-permute-start.3 = (bf16[272,256]{1,0:T(8,128)(2,1)}, bf16[272,256]{1,0:T(8,128)(2,1)}, u32[]{:S(2)}, u32[]{:S(2)}) collective-permute-start(bf16[272,256]{1,0:T(8,128)(2,1)} %fusion.29), channel_id=1, source_target_pairs={{0,4},{2,6},{4,8},{6,10},{8,12},{10,14},{1,5},{3,7},{5,9},{7,11},{... | collective-permute-start | bytes 417800 | tf_op jit(solution)/shard_map/ppermute | solution.py:177
  87.8 2.9 %collective-permute-start.4 = (bf16[272,256]{1,0:T(8,128)(2,1)}, bf16[272,256]{1,0:T(8,128)(2,1)}, u32[]{:S(2)}, u32[]{:S(2)}) collective-permute-start(bf16[272,256]{1,0:T(8,128)(2,1)} %fusion.29), channel_id=1, source_target_pairs={{0,2},{2,4},{4,6},{6,8},{8,10},{10,12},{12,14},{1,3},{3,5},{5,7},{... | collective-permute-start | bytes 417800 | tf_op jit(solution)/shard_map/ppermute | solution.py:177
  91.3 16.5 %all-gather.5.cloned.1.call-done = bf16[8192,256]{1,0:T(8,128)(2,1)} async-done(((bf16[512,256]{1,0:T(8,128)(2,1)}), bf16[8192,256]{1,0:T(8,128)(2,1)}) %all-gather.5.cloned.1.call-update) | async-done | bytes 4194320 | tf_op jit(solution)/shard_map/all_gather | solution.py:145
  107.7 3.1 %fusion.2 = f32[256,256]{0,1:T(8,128)S(1)} fusion(bf16[2,4096,256]{2,1,0:T(8,128)(2,1)} %bitcast.76, s32[]{:T(128)S(6)} %select_n.8, bf16[1,256,4096]{2,1,0:T(8,128)(2,1)} %param.13), kind=kOutput, calls=%fused_computation.3 | convolution fusion | flops 536870912 | bytes 4456452 | tf_op jit(solution)/shard_map/dot_general | solution.py:147
  113.0 5.0 %collective-permute-start.1 = (bf16[144,256]{1,0:T(8,128)(2,1)S(1)}, bf16[144,256]{1,0:T(8,128)(2,1)S(1)}, u32[]{:S(2)}, u32[]{:S(2)}) collective-permute-start(bf16[144,256]{1,0:T(8,128)(2,1)S(1)} %fusion.38), channel_id=1, source_target_pairs={{0,8},{2,10},{4,12},{6,14},{1,9},{3,11},{5,13},{7,15},{16,24},{18,... | collective-permute-start | bytes 221192 | tf_op jit(solution)/shard_map/ppermute | solution.py:177
  118.3 1.4 collective-permute-start.5
  119.7 1.9 collective-permute-done.5
  121.6 10.8 %collective-permute-start.6 = (bf16[256,256]{1,0:T(8,128)(2,1)S(1)}, bf16[256,256]{1,0:T(8,128)(2,1)S(1)}, u32[]{:S(2)}, u32[]{:S(2)}) collective-permute-start(bf16[256,256]{1,0:T(8,128)(2,1)S(1)} %pad_maximum_fusion.3), channel_id=1, source_target_pairs={{0,6},{2,8},{4,10},{6,12},{8,14},{1,7},{3,9},{5,11},{7,13},{9,15},... | collective-permute-start | bytes 393224 | tf_op jit(solution)/shard_map/ppermute | solution.py:177
  132.4 1.9 %collective-permute-start.7 = (bf16[256,256]{1,0:T(8,128)(2,1)S(1)}, bf16[256,256]{1,0:T(8,128)(2,1)S(1)}, u32[]{:S(2)}, u32[]{:S(2)}) collective-permute-start(bf16[256,256]{1,0:T(8,128)(2,1)S(1)} %pad_maximum_fusion.3), channel_id=1, source_target_pairs={{0,4},{2,6},{4,8},{6,10},{8,12},{10,14},{1,5},{3,7},{5,9},{7,11},{... | collective-permute-start | bytes 393224 | tf_op jit(solution)/shard_map/ppermute | solution.py:177
  135.5 6.6 %collective-permute-done.6 = bf16[256,256]{1,0:T(8,128)(2,1)S(1)} collective-permute-done((bf16[256,256]{1,0:T(8,128)(2,1)S(1)}, bf16[256,256]{1,0:T(8,128)(2,1)S(1)}, u32[]{:S(2)}, u32[]{:S(2)}) %collective-permute-start.6) | collective-permute-done | bytes 131104 | tf_op jit(solution)/shard_map/ppermute | solution.py:177
  142.1 2.1 %collective-permute-start.8 = (bf16[256,256]{1,0:T(8,128)(2,1)S(1)}, bf16[256,256]{1,0:T(8,128)(2,1)S(1)}, u32[]{:S(2)}, u32[]{:S(2)}) collective-permute-start(bf16[256,256]{1,0:T(8,128)(2,1)S(1)} %pad_maximum_fusion.3), channel_id=1, source_target_pairs={{0,2},{2,4},{4,6},{6,8},{8,10},{10,12},{12,14},{1,3},{3,5},{5,7},{... | collective-permute-start | bytes 393224 | tf_op jit(solution)/shard_map/ppermute | solution.py:177
  144.9 4.4 %collective-permute-done.8 = bf16[256,256]{1,0:T(8,128)(2,1)S(1)} collective-permute-done((bf16[256,256]{1,0:T(8,128)(2,1)S(1)}, bf16[256,256]{1,0:T(8,128)(2,1)S(1)}, u32[]{:S(2)}, u32[]{:S(2)}) %collective-permute-start.8) | collective-permute-done | bytes 131104 | tf_op jit(solution)/shard_map/ppermute | solution.py:177
  152.2 1.2 fusion.45
  153.4 1.2 fusion.46
  154.6 1.2 fusion.47
  156.6 1.0 and_convert_fusion.vis_ref
  157.6 11.7 %shard_map.55 = bf16[256,2048]{1,0:T(8,128)(2,1)S(1)} custom-call(s32[256,1152]{1,0:T(8,128)S(1)} %and_convert_fusion.vis_ref, f32[256,128]{1,0:T(8,128)S(1)} %get-tuple-element.50.cos_ref, f32[256,128]{1,0:T(8,128)S(1)} %get-tuple-element.51.sin_ref, bf16[256,4096]{1,0:T(8,128)(2,1)S(1)} %bitcast.73, bf16[1152,256]{1,0:T(8,128)(2,1)S(1)} %fusion.30.k_ref.v_ref, ...), custom_call_target="tpu_custom_call" | custom-call | flops 2415919104 | bytes 3866624 | tf_op jit(solution)/shard_map/pallas_call | solution.py:89
  169.3 11.7 %shard_map.56 = bf16[256,2048]{1,0:T(8,128)(2,1)S(1)} custom-call(s32[256,1152]{1,0:T(8,128)S(1)} %and_convert_fusion.vis_ref, f32[256,128]{1,0:T(8,128)S(1)} %get-tuple-element.50.cos_ref, f32[256,128]{1,0:T(8,128)S(1)} %get-tuple-element.51.sin_ref, bf16[256,4096]{1,0:T(8,128)(2,1)S(1)} %bitcast.74, ...), custom_call_target="tpu_custom_call" | custom-call | flops 2415919104 | bytes 3866624 | tf_op jit(solution)/shard_map/pallas_call | solution.py:89
  181.0 1.5 maximum_bitcast_fusion
  (68 shorter events, 13.5 us)
Async XLA Ops:
  6.5 3.3 %copy-start.8 = (s32[1,2]{1,0:T(1,128)S(1)}, s32[1,2]{1,0:T(1,128)}, u32[]{:S(2)}) copy-start(s32[1,2]{1,0:T(1,128)} %param.17) | copy-start | bytes 28
  6.5 58.8 %all-gather.3.cloned.1.call-start = ((), (), s32[]{:S(2)}) async-start(), calls=%async_computation | async-start | bytes 4456448 | tf_op jit(solution)/shard_map/all_gather | solution.py:145
  8.4 99.3 %all-gather.5.cloned.1.call-start = ((), (), s32[]{:S(2)}) async-start(), calls=%async_computation.1 | async-start | bytes 4456448 | tf_op jit(solution)/shard_map/all_gather | solution.py:145
  9.3 68.8 %collective-permute-start = (bf16[256,4096]{1,0:T(8,128)(2,1)}, bf16[256,4096]{1,0:T(8,128)(2,1)S(1)}, u32[]{:S(2)}, u32[]{:S(2)}) collective-permute-start(bf16[256,4096]{1,0:T(8,128)(2,1)} %bitcast.75), channel_id=1, source_target_pairs={{0,1},{1,0},{2,3},{3,2},{4,5},{5,4},{6,7},{7,6},{8,9},{9,8},{10,11... | collective-permute-start | bytes 6291464 | tf_op jit(solution)/shard_map/ppermute | solution.py:135
  65.3 12.8 %copy-start.2 = (bf16[8192,256]{1,0:T(8,128)(2,1)S(1)}, bf16[8192,256]{1,0:T(8,128)(2,1)}, u32[]{:S(2)}) copy-start(bf16[8192,256]{1,0:T(8,128)(2,1)} %all-gather.3.cloned.1.call-done) | copy-start | bytes 12582916
  78.9 12.4 %copy-start.3 = (bf16[256,128]{1,0:T(8,128)(2,1)}, bf16[256,128]{1,0:T(8,128)(2,1)S(1)}, u32[]{:S(2)}) copy-start(bf16[256,128]{1,0:T(8,128)(2,1)S(1)} %slice.213) | copy-start | bytes 196612
  79.2 12.0 %copy-start.5 = (bf16[256,128]{1,0:T(8,128)(2,1)}, bf16[256,128]{1,0:T(8,128)(2,1)S(1)}, u32[]{:S(2)}) copy-start(bf16[256,128]{1,0:T(8,128)(2,1)S(1)} %fusion.34) | copy-start | bytes 196612
  79.9 69.5 %collective-permute-start.2 = (bf16[272,256]{1,0:T(8,128)(2,1)}, bf16[272,256]{1,0:T(8,128)(2,1)}, u32[]{:S(2)}, u32[]{:S(2)}) collective-permute-start(bf16[272,256]{1,0:T(8,128)(2,1)} %fusion.29), channel_id=1, source_target_pairs={{0,6},{2,8},{4,10},{6,12},{8,14},{1,7},{3,9},{5,11},{7,13},{9,15},... | collective-permute-start | bytes 417800 | tf_op jit(solution)/shard_map/ppermute | solution.py:177
  85.8 64.4 %collective-permute-start.3 = (bf16[272,256]{1,0:T(8,128)(2,1)}, bf16[272,256]{1,0:T(8,128)(2,1)}, u32[]{:S(2)}, u32[]{:S(2)}) collective-permute-start(bf16[272,256]{1,0:T(8,128)(2,1)} %fusion.29), channel_id=1, source_target_pairs={{0,4},{2,6},{4,8},{6,10},{8,12},{10,14},{1,5},{3,7},{5,9},{7,11},{... | collective-permute-start | bytes 417800 | tf_op jit(solution)/shard_map/ppermute | solution.py:177
  87.8 63.4 %collective-permute-start.4 = (bf16[272,256]{1,0:T(8,128)(2,1)}, bf16[272,256]{1,0:T(8,128)(2,1)}, u32[]{:S(2)}, u32[]{:S(2)}) collective-permute-start(bf16[272,256]{1,0:T(8,128)(2,1)} %fusion.29), channel_id=1, source_target_pairs={{0,2},{2,4},{4,6},{6,8},{8,10},{10,12},{12,14},{1,3},{3,5},{5,7},{... | collective-permute-start | bytes 417800 | tf_op jit(solution)/shard_map/ppermute | solution.py:177
  107.7 3.7 %copy-start.1 = (bf16[8192,256]{1,0:T(8,128)(2,1)S(1)}, bf16[8192,256]{1,0:T(8,128)(2,1)}, u32[]{:S(2)}) copy-start(bf16[8192,256]{1,0:T(8,128)(2,1)} %all-gather.5.cloned.1.call-done) | copy-start | bytes 12582916
  111.5 6.6 %copy-start.7 = (f32[128]{0:T(128)S(1)}, f32[128]{0:T(128)}, u32[]{:S(2)}) copy-start(f32[128]{0:T(128)} %constant.128.clone.1) | copy-start | bytes 1540
  112.3 39.9 %copy-start.4 = (bf16[256,128]{1,0:T(8,128)(2,1)S(1)}, bf16[256,128]{1,0:T(8,128)(2,1)}, u32[]{:S(2)}) copy-start(bf16[256,128]{1,0:T(8,128)(2,1)} %copy-done.3) | copy-start | bytes 196612
  112.3 39.9 %copy-start.6 = (bf16[256,128]{1,0:T(8,128)(2,1)S(1)}, bf16[256,128]{1,0:T(8,128)(2,1)}, u32[]{:S(2)}) copy-start(bf16[256,128]{1,0:T(8,128)(2,1)} %copy-done.5) | copy-start | bytes 196612
  113.0 19.4 %collective-permute-start.1 = (bf16[144,256]{1,0:T(8,128)(2,1)S(1)}, bf16[144,256]{1,0:T(8,128)(2,1)S(1)}, u32[]{:S(2)}, u32[]{:S(2)}) collective-permute-start(bf16[144,256]{1,0:T(8,128)(2,1)S(1)} %fusion.38), channel_id=1, source_target_pairs={{0,8},{2,10},{4,12},{6,14},{1,9},{3,11},{5,13},{7,15},{16,24},{18,... | collective-permute-start | bytes 221192 | tf_op jit(solution)/shard_map/ppermute | solution.py:177
  118.2 39.4 %copy-start = (bf16[1,256,4096]{2,1,0:T(8,128)(2,1)S(1)}, bf16[1,256,4096]{2,1,0:T(8,128)(2,1)}, u32[]{:S(2)}) copy-start(bf16[1,256,4096]{2,1,0:T(8,128)(2,1)} %param.14) | copy-start | bytes 6291460
  118.3 3.3 %collective-permute-start.5 = (bf16[128,256]{1,0:T(8,128)(2,1)S(1)}, bf16[128,256]{1,0:T(8,128)(2,1)S(1)}, u32[]{:S(2)}, u32[]{:S(2)}) collective-permute-start(bf16[128,256]{1,0:T(8,128)(2,1)S(1)} %fusion.39), channel_id=1, source_target_pairs={{0,8},{2,10},{4,12},{6,14},{1,9},{3,11},{5,13},{7,15},{16,24},{18,... | collective-permute-start | bytes 196616 | tf_op jit(solution)/shard_map/ppermute | solution.py:177
  121.6 20.5 %collective-permute-start.6 = (bf16[256,256]{1,0:T(8,128)(2,1)S(1)}, bf16[256,256]{1,0:T(8,128)(2,1)S(1)}, u32[]{:S(2)}, u32[]{:S(2)}) collective-permute-start(bf16[256,256]{1,0:T(8,128)(2,1)S(1)} %pad_maximum_fusion.3), channel_id=1, source_target_pairs={{0,6},{2,8},{4,10},{6,12},{8,14},{1,7},{3,9},{5,11},{7,13},{9,15},... | collective-permute-start | bytes 393224 | tf_op jit(solution)/shard_map/ppermute | solution.py:177
  132.4 12.5 %collective-permute-start.7 = (bf16[256,256]{1,0:T(8,128)(2,1)S(1)}, bf16[256,256]{1,0:T(8,128)(2,1)S(1)}, u32[]{:S(2)}, u32[]{:S(2)}) collective-permute-start(bf16[256,256]{1,0:T(8,128)(2,1)S(1)} %pad_maximum_fusion.3), channel_id=1, source_target_pairs={{0,4},{2,6},{4,8},{6,10},{8,12},{10,14},{1,5},{3,7},{5,9},{7,11},{... | collective-permute-start | bytes 393224 | tf_op jit(solution)/shard_map/ppermute | solution.py:177
  142.1 7.2 %collective-permute-start.8 = (bf16[256,256]{1,0:T(8,128)(2,1)S(1)}, bf16[256,256]{1,0:T(8,128)(2,1)S(1)}, u32[]{:S(2)}, u32[]{:S(2)}) collective-permute-start(bf16[256,256]{1,0:T(8,128)(2,1)S(1)} %pad_maximum_fusion.3), channel_id=1, source_target_pairs={{0,2},{2,4},{4,6},{6,8},{8,10},{10,12},{12,14},{1,3},{3,5},{5,7},{... | collective-permute-start | bytes 393224 | tf_op jit(solution)/shard_map/ppermute | solution.py:177
Sparse Core Ops, SparseCore 0:
  9.2 56.0 all-gather.2
  67.2 40.5 all-gather.4

commit v2 on v1

--- a/solution.py
+++ b/solution.py
@@ -23,12 +23,16 @@
 
 
 def yarn_tables(positions):
+    return yarn_tables_at(positions.astype(jnp.float32))
+
+
+def yarn_tables_at(float_positions):
     counter = jnp.arange(HD // 2, dtype=jnp.float32)
     base_freq = ROPE_BASE ** (-2.0 * counter / HD)
     wave_ratio = PRETRAIN_CONTEXT * base_freq / (2.0 * math.pi)
     ramp_value = jnp.clip((wave_ratio - BETA_SLOW) / (BETA_FAST - BETA_SLOW), 0.0, 1.0)
     frequency = ramp_value * base_freq + (1.0 - ramp_value) * base_freq / YARN_FACTOR
-    angles = positions.astype(jnp.float32)[:, None] * frequency[None, :]
+    angles = float_positions[:, None] * frequency[None, :]
     cosine = jnp.cos(angles)
     sine_table = jnp.sin(angles)
     return (
@@ -131,7 +135,11 @@
         half_sign = jnp.concatenate(
             [-jnp.ones((HD // 2,), jnp.float32), jnp.ones((HD // 2,), jnp.float32)]
         )
-        signed_sine = sine_table * half_sign[None, :]
+        kernel_positions = jnp.arange(row_count, dtype=jnp.float32) + (ctx_rank * row_count).astype(
+            jnp.float32
+        )
+        kernel_cosine, kernel_sine = yarn_tables_at(kernel_positions)
+        signed_sine = kernel_sine * half_sign[None, :]
         partner_tokens = lax.ppermute(local_tokens, "tp", [(0, 1), (1, 0)])
         local_docs = doc_blocks[0]
         blocks_here = row_count // BLOCK
@@ -198,7 +206,7 @@
                 ).astype(jnp.int32)
             outputs.append(
                 dense_attention(
-                    visible, cosine, signed_sine, query_rot, kv_all, kv_heads, head
+                    visible, kernel_cosine, signed_sine, query_rot, kv_all, kv_heads, head
                 )
             )
         context = jnp.concatenate(outputs, axis=1)

time: 192 us -> 192 us (level)
  transfers between devices with their start and end apart: 11 -> 11, of which waited for: 7 -> 7; matrix products, arithmetic and copies ran while one was open for 8% -> 9% of each run, Pallas kernels for 0% -> 0%
where the time goes in v2:
time: 192 us; the launch traced here: 190 us
  waiting for transfers between devices  92.2 us (48%)
  starting transfers between devices  32.6 us (17%)
  Pallas kernels  23.3 us (12%)
  between operations  15 us (8%)
  other arithmetic  12.2 us (6%)
  matrix products  7.62 us (4%)
  local copies, waits for them, and re-layouts  7.23 us (4%)
    all_gather x2, waiting for transfers between devices, layer(): weights = lax.all_gather(joined, 'dp', axis=0, tiled=True)  68.9 us
    ppermute x8, starting transfers between devices, layer(): arrived = lax.ppermute(payload, 'ctx', pairs)  32 us
    pallas_call x2, Pallas kernels, dense_attention(): pl.pallas_call(dense_kernel, grid=(q_blocks,), in_specs=[pl.BlockSpec((BL...  23.3 us
    ppermute x8, waiting for transfers between devices, layer(): arrived = lax.ppermute(payload, 'ctx', pairs)  13.6 us
    ppermute x1, waiting for transfers between devices, layer(): partner_tokens = lax.ppermute(local_tokens, 'tp', [(0, 1), (1, 0)])  9.71 us
    dot_general x2, matrix products, layer(): jnp.dot(local_tokens, weights[tp_rank], preferred_element_type=jnp.float32)  6.15 us
  transfers between devices with their start and end apart: 11, of which 7 were waited for; matrix products, arithmetic and copies ran while one was open for 9% of the time, Pallas kernels for 0%

profile of v2, /device:TPU:100, one launch (start us, length us, event | category | flops | bytes accessed | tf_op | source)
XLA Modules:
  0.0 190.1 jit_solution(13835289711156038538)
XLA Ops:
  6.5 1.2 fusion.50
  11.8 1.0 multiply_sine_fusion
  12.9 52.4 %all-gather.3.cloned.1.call-done = bf16[8192,256]{1,0:T(8,128)(2,1)} async-done(((bf16[512,256]{1,0:T(8,128)(2,1)}), bf16[8192,256]{1,0:T(8,128)(2,1)}) %all-gather.3.cloned.1.call-update) | async-done | bytes 4194320 | tf_op jit(solution)/shard_map/all_gather | solution.py:153
  65.3 3.1 %fusion.6 = f32[256,256]{0,1:T(8,128)S(1)} fusion(bf16[2,4096,256]{2,1,0:T(8,128)(2,1)} %bitcast.78, s32[]{:T(128)S(6)} %select_n.8, bf16[1,256,4096]{2,1,0:T(8,128)(2,1)} %param.13), kind=kOutput, calls=%fused_computation.7 | convolution fusion | flops 536870912 | bytes 4456452 | tf_op jit(solution)/shard_map/dot_general | solution.py:155
  68.4 9.7 %collective-permute-done = bf16[256,4096]{1,0:T(8,128)(2,1)S(1)} collective-permute-done((bf16[256,4096]{1,0:T(8,128)(2,1)}, bf16[256,4096]{1,0:T(8,128)(2,1)S(1)}, u32[]{:S(2)}, u32[]{:S(2)}) %collective-permute-start) | collective-permute-done | bytes 2097184 | tf_op jit(solution)/shard_map/ppermute | solution.py:143
  79.9 5.9 %collective-permute-start.2 = (bf16[272,256]{1,0:T(8,128)(2,1)}, bf16[272,256]{1,0:T(8,128)(2,1)}, u32[]{:S(2)}, u32[]{:S(2)}) collective-permute-start(bf16[272,256]{1,0:T(8,128)(2,1)} %fusion.29), channel_id=1, source_target_pairs={{0,6},{2,8},{4,10},{6,12},{8,14},{1,7},{3,9},{5,11},{7,13},{9,15},... | collective-permute-start | bytes 417800 | tf_op jit(solution)/shard_map/ppermute | solution.py:185
  85.8 1.9 %collective-permute-start.3 = (bf16[272,256]{1,0:T(8,128)(2,1)}, bf16[272,256]{1,0:T(8,128)(2,1)}, u32[]{:S(2)}, u32[]{:S(2)}) collective-permute-start(bf16[272,256]{1,0:T(8,128)(2,1)} %fusion.29), channel_id=1, source_target_pairs={{0,4},{2,6},{4,8},{6,10},{8,12},{10,14},{1,5},{3,7},{5,9},{7,11},{... | collective-permute-start | bytes 417800 | tf_op jit(solution)/shard_map/ppermute | solution.py:185
  87.7 2.9 %collective-permute-start.4 = (bf16[272,256]{1,0:T(8,128)(2,1)}, bf16[272,256]{1,0:T(8,128)(2,1)}, u32[]{:S(2)}, u32[]{:S(2)}) collective-permute-start(bf16[272,256]{1,0:T(8,128)(2,1)} %fusion.29), channel_id=1, source_target_pairs={{0,2},{2,4},{4,6},{6,8},{8,10},{10,12},{12,14},{1,3},{3,5},{5,7},{... | collective-permute-start | bytes 417800 | tf_op jit(solution)/shard_map/ppermute | solution.py:185
  91.3 16.5 %all-gather.5.cloned.1.call-done = bf16[8192,256]{1,0:T(8,128)(2,1)} async-done(((bf16[512,256]{1,0:T(8,128)(2,1)}), bf16[8192,256]{1,0:T(8,128)(2,1)}) %all-gather.5.cloned.1.call-update) | async-done | bytes 4194320 | tf_op jit(solution)/shard_map/all_gather | solution.py:153
  107.7 3.1 %fusion.2 = f32[256,256]{0,1:T(8,128)S(1)} fusion(bf16[2,4096,256]{2,1,0:T(8,128)(2,1)} %bitcast.76, s32[]{:T(128)S(6)} %select_n.8, bf16[1,256,4096]{2,1,0:T(8,128)(2,1)} %param.13), kind=kOutput, calls=%fused_computation.3 | convolution fusion | flops 536870912 | bytes 4456452 | tf_op jit(solution)/shard_map/dot_general | solution.py:155
  112.9 5.0 %collective-permute-start.1 = (bf16[144,256]{1,0:T(8,128)(2,1)S(1)}, bf16[144,256]{1,0:T(8,128)(2,1)S(1)}, u32[]{:S(2)}, u32[]{:S(2)}) collective-permute-start(bf16[144,256]{1,0:T(8,128)(2,1)S(1)} %fusion.37), channel_id=1, source_target_pairs={{0,8},{2,10},{4,12},{6,14},{1,9},{3,11},{5,13},{7,15},{16,24},{18,... | collective-permute-start | bytes 221192 | tf_op jit(solution)/shard_map/ppermute | solution.py:185
  118.2 1.4 collective-permute-start.5
  119.7 1.9 collective-permute-done.5
  121.5 10.8 %collective-permute-start.6 = (bf16[256,256]{1,0:T(8,128)(2,1)S(1)}, bf16[256,256]{1,0:T(8,128)(2,1)S(1)}, u32[]{:S(2)}, u32[]{:S(2)}) collective-permute-start(bf16[256,256]{1,0:T(8,128)(2,1)S(1)} %pad_maximum_fusion.3), channel_id=1, source_target_pairs={{0,6},{2,8},{4,10},{6,12},{8,14},{1,7},{3,9},{5,11},{7,13},{9,15},... | collective-permute-start | bytes 393224 | tf_op jit(solution)/shard_map/ppermute | solution.py:185
  132.3 1.9 %collective-permute-start.7 = (bf16[256,256]{1,0:T(8,128)(2,1)S(1)}, bf16[256,256]{1,0:T(8,128)(2,1)S(1)}, u32[]{:S(2)}, u32[]{:S(2)}) collective-permute-start(bf16[256,256]{1,0:T(8,128)(2,1)S(1)} %pad_maximum_fusion.3), channel_id=1, source_target_pairs={{0,4},{2,6},{4,8},{6,10},{8,12},{10,14},{1,5},{3,7},{5,9},{7,11},{... | collective-permute-start | bytes 393224 | tf_op jit(solution)/shard_map/ppermute | solution.py:185
  135.5 6.6 %collective-permute-done.6 = bf16[256,256]{1,0:T(8,128)(2,1)S(1)} collective-permute-done((bf16[256,256]{1,0:T(8,128)(2,1)S(1)}, bf16[256,256]{1,0:T(8,128)(2,1)S(1)}, u32[]{:S(2)}, u32[]{:S(2)}) %collective-permute-start.6) | collective-permute-done | bytes 131104 | tf_op jit(solution)/shard_map/ppermute | solution.py:185
  142.1 2.1 %collective-permute-start.8 = (bf16[256,256]{1,0:T(8,128)(2,1)S(1)}, bf16[256,256]{1,0:T(8,128)(2,1)S(1)}, u32[]{:S(2)}, u32[]{:S(2)}) collective-permute-start(bf16[256,256]{1,0:T(8,128)(2,1)S(1)} %pad_maximum_fusion.3), channel_id=1, source_target_pairs={{0,2},{2,4},{4,6},{6,8},{8,10},{10,12},{12,14},{1,3},{3,5},{5,7},{... | collective-permute-start | bytes 393224 | tf_op jit(solution)/shard_map/ppermute | solution.py:185
  144.9 4.4 %collective-permute-done.8 = bf16[256,256]{1,0:T(8,128)(2,1)S(1)} collective-permute-done((bf16[256,256]{1,0:T(8,128)(2,1)S(1)}, bf16[256,256]{1,0:T(8,128)(2,1)S(1)}, u32[]{:S(2)}, u32[]{:S(2)}) %collective-permute-start.8) | collective-permute-done | bytes 131104 | tf_op jit(solution)/shard_map/ppermute | solution.py:185
  149.3 1.2 fusion.46
  150.6 1.2 fusion.45
  151.8 1.2 fusion.44
  158.5 11.6 %shard_map.56 = bf16[256,2048]{1,0:T(8,128)(2,1)S(1)} custom-call(s32[256,1152]{1,0:T(8,128)S(1)} %and_convert_fusion.vis_ref, f32[256,128]{1,0:T(8,128)S(1)} %get-tuple-element.61.cos_ref, f32[256,128]{1,0:T(8,128)S(1)} %get-tuple-element.62.sin_ref, bf16[256,4096]{1,0:T(8,128)(2,1)S(1)} %bitcast.73, ...), custom_call_target="tpu_custom_call" | custom-call | flops 2415919104 | bytes 3866624 | tf_op jit(solution)/shard_map/pallas_call | solution.py:93
  170.1 11.6 %shard_map.55 = bf16[256,2048]{1,0:T(8,128)(2,1)S(1)} custom-call(s32[256,1152]{1,0:T(8,128)S(1)} %and_convert_fusion.vis_ref, f32[256,128]{1,0:T(8,128)S(1)} %get-tuple-element.61.cos_ref, f32[256,128]{1,0:T(8,128)S(1)} %get-tuple-element.62.sin_ref, bf16[256,4096]{1,0:T(8,128)(2,1)S(1)} %bitcast.74, bf16[1152,256]{1,0:T(8,128)(2,1)S(1)} %fusion.30.k_ref.v_ref, ...), custom_call_target="tpu_custom_call" | custom-call | flops 2415919104 | bytes 3866624 | tf_op jit(solution)/shard_map/pallas_call | solution.py:93
  181.7 1.5 maximum_bitcast_fusion
  (66 shorter events, 15.0 us)
Async XLA Ops:
  6.5 6.2 %copy-start.5 = (f32[128]{0:T(128)S(1)}, f32[128]{0:T(128)}, u32[]{:S(2)}) copy-start(f32[128]{0:T(128)} %constant.128.clone.1) | copy-start | bytes 1540
  6.5 3.3 %copy-start.6 = (s32[1,2]{1,0:T(1,128)S(1)}, s32[1,2]{1,0:T(1,128)}, u32[]{:S(2)}) copy-start(s32[1,2]{1,0:T(1,128)} %param.17) | copy-start | bytes 28
  6.5 58.8 %all-gather.3.cloned.1.call-start = ((), (), s32[]{:S(2)}) async-start(), calls=%async_computation | async-start | bytes 4456448 | tf_op jit(solution)/shard_map/all_gather | solution.py:153
  8.5 99.3 %all-gather.5.cloned.1.call-start = ((), (), s32[]{:S(2)}) async-start(), calls=%async_computation.1 | async-start | bytes 4456448 | tf_op jit(solution)/shard_map/all_gather | solution.py:153
  9.3 68.8 %collective-permute-start = (bf16[256,4096]{1,0:T(8,128)(2,1)}, bf16[256,4096]{1,0:T(8,128)(2,1)S(1)}, u32[]{:S(2)}, u32[]{:S(2)}) collective-permute-start(bf16[256,4096]{1,0:T(8,128)(2,1)} %bitcast.75), channel_id=1, source_target_pairs={{0,1},{1,0},{2,3},{3,2},{4,5},{5,4},{6,7},{7,6},{8,9},{9,8},{10,11... | collective-permute-start | bytes 6291464 | tf_op jit(solution)/shard_map/ppermute | solution.py:143
  65.3 12.8 %copy-start.2 = (bf16[8192,256]{1,0:T(8,128)(2,1)S(1)}, bf16[8192,256]{1,0:T(8,128)(2,1)}, u32[]{:S(2)}) copy-start(bf16[8192,256]{1,0:T(8,128)(2,1)} %all-gather.3.cloned.1.call-done) | copy-start | bytes 12582916
  78.9 12.4 %copy-start.3 = (bf16[256,128]{1,0:T(8,128)(2,1)}, bf16[256,128]{1,0:T(8,128)(2,1)S(1)}, u32[]{:S(2)}) copy-start(bf16[256,128]{1,0:T(8,128)(2,1)S(1)} %slice.213) | copy-start | bytes 196612
  79.2 12.1 %copy-start.4 = (bf16[256,128]{1,0:T(8,128)(2,1)}, bf16[256,128]{1,0:T(8,128)(2,1)S(1)}, u32[]{:S(2)}) copy-start(bf16[256,128]{1,0:T(8,128)(2,1)S(1)} %fusion.34) | copy-start | bytes 196612
  79.9 69.5 %collective-permute-start.2 = (bf16[272,256]{1,0:T(8,128)(2,1)}, bf16[272,256]{1,0:T(8,128)(2,1)}, u32[]{:S(2)}, u32[]{:S(2)}) collective-permute-start(bf16[272,256]{1,0:T(8,128)(2,1)} %fusion.29), channel_id=1, source_target_pairs={{0,6},{2,8},{4,10},{6,12},{8,14},{1,7},{3,9},{5,11},{7,13},{9,15},... | collective-permute-start | bytes 417800 | tf_op jit(solution)/shard_map/ppermute | solution.py:185
  85.8 64.8 %collective-permute-start.3 = (bf16[272,256]{1,0:T(8,128)(2,1)}, bf16[272,256]{1,0:T(8,128)(2,1)}, u32[]{:S(2)}, u32[]{:S(2)}) collective-permute-start(bf16[272,256]{1,0:T(8,128)(2,1)} %fusion.29), channel_id=1, source_target_pairs={{0,4},{2,6},{4,8},{6,10},{8,12},{10,14},{1,5},{3,7},{5,9},{7,11},{... | collective-permute-start | bytes 417800 | tf_op jit(solution)/shard_map/ppermute | solution.py:185
  87.7 64.1 %collective-permute-start.4 = (bf16[272,256]{1,0:T(8,128)(2,1)}, bf16[272,256]{1,0:T(8,128)(2,1)}, u32[]{:S(2)}, u32[]{:S(2)}) collective-permute-start(bf16[272,256]{1,0:T(8,128)(2,1)} %fusion.29), channel_id=1, source_target_pairs={{0,2},{2,4},{4,6},{6,8},{8,10},{10,12},{12,14},{1,3},{3,5},{5,7},{... | collective-permute-start | bytes 417800 | tf_op jit(solution)/shard_map/ppermute | solution.py:185
  107.7 3.7 %copy-start.1 = (bf16[8192,256]{1,0:T(8,128)(2,1)S(1)}, bf16[8192,256]{1,0:T(8,128)(2,1)}, u32[]{:S(2)}) copy-start(bf16[8192,256]{1,0:T(8,128)(2,1)} %all-gather.5.cloned.1.call-done) | copy-start | bytes 12582916
  112.9 19.4 %collective-permute-start.1 = (bf16[144,256]{1,0:T(8,128)(2,1)S(1)}, bf16[144,256]{1,0:T(8,128)(2,1)S(1)}, u32[]{:S(2)}, u32[]{:S(2)}) collective-permute-start(bf16[144,256]{1,0:T(8,128)(2,1)S(1)} %fusion.37), channel_id=1, source_target_pairs={{0,8},{2,10},{4,12},{6,14},{1,9},{3,11},{5,13},{7,15},{16,24},{18,... | collective-permute-start | bytes 221192 | tf_op jit(solution)/shard_map/ppermute | solution.py:185
  118.2 40.3 %copy-start = (bf16[1,256,4096]{2,1,0:T(8,128)(2,1)S(1)}, bf16[1,256,4096]{2,1,0:T(8,128)(2,1)}, u32[]{:S(2)}) copy-start(bf16[1,256,4096]{2,1,0:T(8,128)(2,1)} %param.14) | copy-start | bytes 6291460
  118.2 3.3 %collective-permute-start.5 = (bf16[128,256]{1,0:T(8,128)(2,1)S(1)}, bf16[128,256]{1,0:T(8,128)(2,1)S(1)}, u32[]{:S(2)}, u32[]{:S(2)}) collective-permute-start(bf16[128,256]{1,0:T(8,128)(2,1)S(1)} %fusion.38), channel_id=1, source_target_pairs={{0,8},{2,10},{4,12},{6,14},{1,9},{3,11},{5,13},{7,15},{16,24},{18,... | collective-permute-start | bytes 196616 | tf_op jit(solution)/shard_map/ppermute | solution.py:185
  121.5 20.5 %collective-permute-start.6 = (bf16[256,256]{1,0:T(8,128)(2,1)S(1)}, bf16[256,256]{1,0:T(8,128)(2,1)S(1)}, u32[]{:S(2)}, u32[]{:S(2)}) collective-permute-start(bf16[256,256]{1,0:T(8,128)(2,1)S(1)} %pad_maximum_fusion.3), channel_id=1, source_target_pairs={{0,6},{2,8},{4,10},{6,12},{8,14},{1,7},{3,9},{5,11},{7,13},{9,15},... | collective-permute-start | bytes 393224 | tf_op jit(solution)/shard_map/ppermute | solution.py:185
  132.3 12.6 %collective-permute-start.7 = (bf16[256,256]{1,0:T(8,128)(2,1)S(1)}, bf16[256,256]{1,0:T(8,128)(2,1)S(1)}, u32[]{:S(2)}, u32[]{:S(2)}) collective-permute-start(bf16[256,256]{1,0:T(8,128)(2,1)S(1)} %pad_maximum_fusion.3), channel_id=1, source_target_pairs={{0,4},{2,6},{4,8},{6,10},{8,12},{10,14},{1,5},{3,7},{5,9},{7,11},{... | collective-permute-start | bytes 393224 | tf_op jit(solution)/shard_map/ppermute | solution.py:185
  142.1 7.2 %collective-permute-start.8 = (bf16[256,256]{1,0:T(8,128)(2,1)S(1)}, bf16[256,256]{1,0:T(8,128)(2,1)S(1)}, u32[]{:S(2)}, u32[]{:S(2)}) collective-permute-start(bf16[256,256]{1,0:T(8,128)(2,1)S(1)} %pad_maximum_fusion.3), channel_id=1, source_target_pairs={{0,2},{2,4},{4,6},{6,8},{8,10},{10,12},{12,14},{1,3},{3,5},{5,7},{... | collective-permute-start | bytes 393224 | tf_op jit(solution)/shard_map/ppermute | solution.py:185
Sparse Core Ops, SparseCore 0:
  9.2 56.0 all-gather.2
  67.2 40.5 all-gather.4

commit v3 on v2

--- a/solution.py
+++ b/solution.py
@@ -117,7 +117,18 @@
     return [(i, i + step) for i in range(count - step)]
 
 
-def make_body(n_ctx):
+def x_shift_pairs(n_dp, n_tp, direction):
+    pairs = []
+    for dp in range(n_dp):
+        for tp in range(n_tp):
+            core, x_lo, y = dp % 2, (dp // 2) % 2, dp // 4
+            moved = (2 * tp + x_lo + direction) % (2 * n_tp)
+            target = ((y * 2 + moved % 2) * 2 + core) * n_tp + moved // 2
+            pairs.append((dp * n_tp + tp, target))
+    return pairs
+
+
+def make_body(n_dp, n_ctx, n_tp):
     def body(tokens, queries, k_weight, v_weight, doc_blocks):
         return layer(tokens, queries, k_weight, v_weight, doc_blocks)
 
@@ -140,7 +151,14 @@
         )
         kernel_cosine, kernel_sine = yarn_tables_at(kernel_positions)
         signed_sine = kernel_sine * half_sign[None, :]
-        partner_tokens = lax.ppermute(local_tokens, "tp", [(0, 1), (1, 0)])
+        half_rows = row_count // 2
+        forward = x_shift_pairs(n_dp, n_tp, 1)
+        backward = x_shift_pairs(n_dp, n_tp, -1)
+        via_next = lax.ppermute(local_tokens[:half_rows], ("dp", "tp"), forward)
+        via_prev = lax.ppermute(local_tokens[half_rows:], ("dp", "tp"), backward)
+        via_next = lax.ppermute(via_next, ("dp", "tp"), forward)
+        via_prev = lax.ppermute(via_prev, ("dp", "tp"), backward)
+        partner_tokens = jnp.concatenate([via_next, via_prev], axis=0)
         local_docs = doc_blocks[0]
         blocks_here = row_count // BLOCK
 
@@ -224,7 +242,7 @@
         P("dp", "ctx"),
     )
     return jax.shard_map(
-        make_body(mesh.shape["ctx"]),
+        make_body(mesh.shape["dp"], mesh.shape["ctx"], mesh.shape["tp"]),
         mesh=mesh,
         in_specs=placed,
         out_specs=P("dp", "ctx", "tp"),

time: 192 us -> 190 us (0.990)
  waiting for transfers between devices: 92.2 us -> 76.2 us
  starting transfers between devices: 32.6 us -> 39.8 us
  local copies, waits for them, and re-layouts: 7.23 us -> 12.2 us
  matrix products: 7.62 us -> 9.57 us
    all_gather x2, waiting for transfers between devices: 68.9 us -> 4.72 us  [layer(): weights = lax.all_gather(joined, 'dp', axis=0, tiled=True)]
    ppermute x1 -> x4, waiting for transfers between devices: 9.71 us -> 58.5 us  [the longest x1 34.2 us: layer(): via_next = lax.ppermute(local_tokens[:half_rows], ('dp', 'tp'), forward)]
    ppermute x1 -> x4, starting transfers between devices: 0.59 us -> 4.51 us  [the longest x1 2.48 us: layer(): via_next = lax.ppermute(via_next, ('dp', 'tp'), forward)]
    ppermute x8, starting transfers between devices: 32 us -> 35.3 us  [layer(): arrived = lax.ppermute(payload, 'ctx', pairs)]
    dot_general x2, matrix products: 1.47 us -> 4.64 us  [layer(): jnp.dot(partner_tokens, weights[1 - tp_rank], preferred_element_type=jnp....]
    unnamed x22 -> x29, local copies, waits for them, and re-layouts: 2.82 us -> 5.62 us
  transfers between devices with their start and end apart: 11 -> 14, of which waited for: 7 -> 7; matrix products, arithmetic and copies ran while one was open for 9% -> 12% of each run, Pallas kernels for 0% -> 0%
where the time goes in v3:
time: 190 us; the launch traced here: 188 us
  waiting for transfers between devices  76.2 us (40%)
  starting transfers between devices  39.8 us (21%)
  Pallas kernels  23.3 us (12%)
  between operations  15 us (8%)
  local copies, waits for them, and re-layouts  12.2 us (6%)
  other arithmetic  11.4 us (6%)
  matrix products  9.57 us (5%)
    ppermute x8, starting transfers between devices, layer(): arrived = lax.ppermute(payload, 'ctx', pairs)  35.3 us
    ppermute x1, waiting for transfers between devices, layer(): via_next = lax.ppermute(local_tokens[:half_rows], ('dp', 'tp'), forward)  34.2 us
    ppermute x1, waiting for transfers between devices, layer(): via_next = lax.ppermute(via_next, ('dp', 'tp'), forward)  24.3 us
    pallas_call x2, Pallas kernels, dense_attention(): pl.pallas_call(dense_kernel, grid=(q_blocks,), in_specs=[pl.BlockSpec((BL...  23.3 us
    ppermute x8, waiting for transfers between devices, layer(): arrived = lax.ppermute(payload, 'ctx', pairs)  12.9 us
    unnamed x29, local copies, waits for them, and re-layouts  5.62 us
    dot_general x2, matrix products, layer(): jnp.dot(local_tokens, weights[tp_rank], preferred_element_type=jnp.float32)  4.93 us
    all_gather x2, waiting for transfers between devices, layer(): weights = lax.all_gather(joined, 'dp', axis=0, tiled=True)  4.72 us
  transfers between devices with their start and end apart: 14, of which 7 were waited for; matrix products, arithmetic and copies ran while one was open for 12% of the time, Pallas kernels for 0%

profile of v3, /device:TPU:100, one launch (start us, length us, event | category | flops | bytes accessed | tf_op | source)
XLA Modules:
  0.0 187.6 jit_solution(17776069566890923828)
XLA Ops:
  6.5 1.3 fusion.54
  13.2 34.2 %collective-permute-done = bf16[128,4096]{1,0:T(8,128)(2,1)} collective-permute-done((bf16[128,4096]{1,0:T(8,128)(2,1)}, bf16[128,4096]{1,0:T(8,128)(2,1)}, u32[]{:S(2)}, u32[]{:S(2)}) %collective-permute-start) | collective-permute-done | bytes 1048608 | tf_op jit(solution)/shard_map/ppermute | solution.py:157
  47.3 2.5 %collective-permute-start.1 = (bf16[128,4096]{1,0:T(8,128)(2,1)}, bf16[128,4096]{1,0:T(8,128)(2,1)}, u32[]{:S(2)}, u32[]{:S(2)}) collective-permute-start(bf16[128,4096]{1,0:T(8,128)(2,1)} %collective-permute-done), channel_id=1, source_target_pairs={{0,32},{1,33},{16,48},{17,49},{32,1},{33,0},{48,17},{49,16},{64,96... | collective-permute-start | bytes 3145736 | tf_op jit(solution)/shard_map/ppermute | solution.py:159
  52.3 24.3 %collective-permute-done.1 = bf16[128,4096]{1,0:T(8,128)(2,1)} collective-permute-done((bf16[128,4096]{1,0:T(8,128)(2,1)}, bf16[128,4096]{1,0:T(8,128)(2,1)}, u32[]{:S(2)}, u32[]{:S(2)}) %collective-permute-start.1) | collective-permute-done | bytes 1048608 | tf_op jit(solution)/shard_map/ppermute | solution.py:159
  76.6 2.3 %constant_dynamic-update-slice_fusion.1 = bf16[256,4096]{1,0:T(8,128)(2,1)} fusion(bf16[128,4096]{1,0:T(8,128)(2,1)} %collective-permute-done.1), kind=kLoop, calls=%fused_computation.69 | loop fusion | bytes 2097152
  80.0 2.5 %fusion.14 = f32[256,256]{1,0:T(8,128)S(1)} fusion(bf16[2,4096,256]{2,1,0:T(8,128)(2,1)} %bitcast.85, s32[]{:T(128)S(6)} %select_n.8, bf16[1,256,4096]{2,1,0:T(8,128)(2,1)S(1)} %copy-done.1), kind=kOutput, calls=%fused_computation.16 | convolution fusion | flops 536870912 | bytes 4456452 | tf_op jit(solution)/shard_map/dot_general | solution.py:173
  82.9 2.3 %fusion.19 = f32[256,256]{1,0:T(8,128)S(1)} fusion(f32[256,256]{1,0:T(8,128)S(1)} %fusion.14, bf16[256,4096]{1,0:T(8,128)(2,1)} %constant_dynamic-update-slice_fusion, bf16[2,4096,256]{2,1,0:T(8,128)(2,1)S(1)} %bitcast.86, s32[]{:T(128)S(6)} %select_n.9), kind=kOutput, calls=%fused_computation.17 | convolution fusion | flops 536936448 | bytes 4718596 | tf_op jit(solution)/shard_map/dot_general | solution.py:174
  86.3 7.3 %collective-permute-start.5 = (bf16[272,256]{1,0:T(8,128)(2,1)}, bf16[272,256]{1,0:T(8,128)(2,1)}, u32[]{:S(2)}, u32[]{:S(2)}) collective-permute-start(bf16[272,256]{1,0:T(8,128)(2,1)} %fusion.35), channel_id=1, source_target_pairs={{0,6},{2,8},{4,10},{6,12},{8,14},{1,7},{3,9},{5,11},{7,13},{9,15},... | collective-permute-start | bytes 417800 | tf_op jit(solution)/shard_map/ppermute | solution.py:203
  93.6 1.9 %collective-permute-start.6 = (bf16[272,256]{1,0:T(8,128)(2,1)}, bf16[272,256]{1,0:T(8,128)(2,1)}, u32[]{:S(2)}, u32[]{:S(2)}) collective-permute-start(bf16[272,256]{1,0:T(8,128)(2,1)} %fusion.35), channel_id=1, source_target_pairs={{0,4},{2,6},{4,8},{6,10},{8,12},{10,14},{1,5},{3,7},{5,9},{7,11},{... | collective-permute-start | bytes 417800 | tf_op jit(solution)/shard_map/ppermute | solution.py:203
  95.6 3.7 %collective-permute-start.7 = (bf16[272,256]{1,0:T(8,128)(2,1)}, bf16[272,256]{1,0:T(8,128)(2,1)}, u32[]{:S(2)}, u32[]{:S(2)}) collective-permute-start(bf16[272,256]{1,0:T(8,128)(2,1)} %fusion.35), channel_id=1, source_target_pairs={{0,2},{2,4},{4,6},{6,8},{8,10},{10,12},{12,14},{1,3},{3,5},{5,7},{... | collective-permute-start | bytes 417800 | tf_op jit(solution)/shard_map/ppermute | solution.py:203
  99.8 4.7 %all-gather.5.cloned.1.call-done = bf16[8192,256]{1,0:T(8,128)(2,1)} async-done(((bf16[512,256]{1,0:T(8,128)(2,1)}), bf16[8192,256]{1,0:T(8,128)(2,1)}) %all-gather.5.cloned.1.call-update) | async-done | bytes 4194320 | tf_op jit(solution)/shard_map/all_gather | solution.py:171
  104.5 2.4 %fusion.22 = f32[256,256]{1,0:T(8,128)S(1)} fusion(bf16[2,4096,256]{2,1,0:T(8,128)(2,1)} %bitcast.83, s32[]{:T(128)S(6)} %select_n.8, bf16[1,256,4096]{2,1,0:T(8,128)(2,1)S(1)} %copy-done.1), kind=kOutput, calls=%fused_computation.18 | convolution fusion | flops 536870912 | bytes 4456452 | tf_op jit(solution)/shard_map/dot_general | solution.py:173
  107.5 2.3 %fusion.30 = f32[256,256]{1,0:T(8,128)S(1)} fusion(f32[256,256]{1,0:T(8,128)S(1)} %fusion.22, bf16[256,4096]{1,0:T(8,128)(2,1)} %constant_dynamic-update-slice_fusion, bf16[2,4096,256]{2,1,0:T(8,128)(2,1)S(1)} %bitcast.84, s32[]{:T(128)S(6)} %select_n.9, f32[]{:T(128)} %bitcast.22), kind=kOutput, calls=%fused_computation.20 | convolution fusion | flops 537001984 | bytes 4718600 | tf_op jit(solution)/shard_map/dot_general | solution.py:174
  110.6 6.5 %collective-permute-start.4 = (bf16[144,256]{1,0:T(8,128)(2,1)S(1)}, bf16[144,256]{1,0:T(8,128)(2,1)S(1)}, u32[]{:S(2)}, u32[]{:S(2)}) collective-permute-start(bf16[144,256]{1,0:T(8,128)(2,1)S(1)} %fusion.43), channel_id=1, source_target_pairs={{0,8},{2,10},{4,12},{6,14},{1,9},{3,11},{5,13},{7,15},{16,24},{18,... | collective-permute-start | bytes 221192 | tf_op jit(solution)/shard_map/ppermute | solution.py:203
  117.4 1.4 collective-permute-start.8
  118.9 1.9 collective-permute-done.8
  120.7 10.4 %collective-permute-start.9 = (bf16[256,256]{1,0:T(8,128)(2,1)S(1)}, bf16[256,256]{1,0:T(8,128)(2,1)S(1)}, u32[]{:S(2)}, u32[]{:S(2)}) collective-permute-start(bf16[256,256]{1,0:T(8,128)(2,1)S(1)} %pad_maximum_fusion.3), channel_id=1, source_target_pairs={{0,6},{2,8},{4,10},{6,12},{8,14},{1,7},{3,9},{5,11},{7,13},{9,15},... | collective-permute-start | bytes 393224 | tf_op jit(solution)/shard_map/ppermute | solution.py:203
  131.2 1.9 %collective-permute-start.10 = (bf16[256,256]{1,0:T(8,128)(2,1)S(1)}, bf16[256,256]{1,0:T(8,128)(2,1)S(1)}, u32[]{:S(2)}, u32[]{:S(2)}) collective-permute-start(bf16[256,256]{1,0:T(8,128)(2,1)S(1)} %pad_maximum_fusion.3), channel_id=1, source_target_pairs={{0,4},{2,6},{4,8},{6,10},{8,12},{10,14},{1,5},{3,7},{5,9},{7,11},{... | collective-permute-start | bytes 393224 | tf_op jit(solution)/shard_map/ppermute | solution.py:203
  134.3 6.0 %collective-permute-done.9 = bf16[256,256]{1,0:T(8,128)(2,1)S(1)} collective-permute-done((bf16[256,256]{1,0:T(8,128)(2,1)S(1)}, bf16[256,256]{1,0:T(8,128)(2,1)S(1)}, u32[]{:S(2)}, u32[]{:S(2)}) %collective-permute-start.9) | collective-permute-done | bytes 131104 | tf_op jit(solution)/shard_map/ppermute | solution.py:203
  140.3 2.1 %collective-permute-start.11 = (bf16[256,256]{1,0:T(8,128)(2,1)S(1)}, bf16[256,256]{1,0:T(8,128)(2,1)S(1)}, u32[]{:S(2)}, u32[]{:S(2)}) collective-permute-start(bf16[256,256]{1,0:T(8,128)(2,1)S(1)} %pad_maximum_fusion.3), channel_id=1, source_target_pairs={{0,2},{2,4},{4,6},{6,8},{8,10},{10,12},{12,14},{1,3},{3,5},{5,7},{... | collective-permute-start | bytes 393224 | tf_op jit(solution)/shard_map/ppermute | solution.py:203
  143.1 4.3 %collective-permute-done.11 = bf16[256,256]{1,0:T(8,128)(2,1)S(1)} collective-permute-done((bf16[256,256]{1,0:T(8,128)(2,1)S(1)}, bf16[256,256]{1,0:T(8,128)(2,1)S(1)}, u32[]{:S(2)}, u32[]{:S(2)}) %collective-permute-start.11) | collective-permute-done | bytes 131104 | tf_op jit(solution)/shard_map/ppermute | solution.py:203
  155.9 11.7 %shard_map.55 = bf16[256,2048]{1,0:T(8,128)(2,1)S(1)} custom-call(s32[256,1152]{1,0:T(8,128)S(1)} %and_convert_fusion.vis_ref, f32[256,128]{1,0:T(8,128)S(1)} %get-tuple-element.63.cos_ref, f32[256,128]{1,0:T(8,128)S(1)} %get-tuple-element.64.sin_ref, bf16[256,4096]{1,0:T(8,128)(2,1)S(1)} %bitcast.81, bf16[1152,256]{1,0:T(8,128)(2,1)S(1)} %fusion.36.k_ref.v_ref, ...), custom_call_target="tpu_custom_call" | custom-call | flops 2415919104 | bytes 3866624 | tf_op jit(solution)/shard_map/pallas_call | solution.py:93
  167.5 11.7 %shard_map.56 = bf16[256,2048]{1,0:T(8,128)(2,1)S(1)} custom-call(s32[256,1152]{1,0:T(8,128)S(1)} %and_convert_fusion.vis_ref, f32[256,128]{1,0:T(8,128)S(1)} %get-tuple-element.63.cos_ref, f32[256,128]{1,0:T(8,128)S(1)} %get-tuple-element.64.sin_ref, bf16[256,4096]{1,0:T(8,128)(2,1)S(1)} %bitcast.82, ...), custom_call_target="tpu_custom_call" | custom-call | flops 2415919104 | bytes 3866624 | tf_op jit(solution)/shard_map/pallas_call | solution.py:93
  179.2 1.5 maximum_bitcast_fusion
  (81 shorter events, 21.3 us)
Async XLA Ops:
  6.5 2.8 %copy-start.1 = (bf16[1,256,4096]{2,1,0:T(8,128)(2,1)S(1)}, bf16[1,256,4096]{2,1,0:T(8,128)(2,1)}, u32[]{:S(2)}) copy-start(bf16[1,256,4096]{2,1,0:T(8,128)(2,1)} %param.13) | copy-start | bytes 6291460
  6.5 73.4 %all-gather.3.cloned.1.call-start = ((), (), s32[]{:S(2)}) async-start(), calls=%async_computation | async-start | bytes 4456448 | tf_op jit(solution)/shard_map/all_gather | solution.py:171
  8.6 95.9 %all-gather.5.cloned.1.call-start = ((), (), s32[]{:S(2)}) async-start(), calls=%async_computation.1 | async-start | bytes 4456448 | tf_op jit(solution)/shard_map/all_gather | solution.py:171
  9.4 40.4 %copy-start.9 = (s32[1,2]{1,0:T(1,128)S(1)}, s32[1,2]{1,0:T(1,128)}, u32[]{:S(2)}) copy-start(s32[1,2]{1,0:T(1,128)} %param.17) | copy-start | bytes 28
  9.4 42.7 %copy-start.8 = (f32[128]{0:T(128)S(1)}, f32[128]{0:T(128)}, u32[]{:S(2)}) copy-start(f32[128]{0:T(128)} %constant.128.clone.1) | copy-start | bytes 1540
  10.5 36.8 %collective-permute-start = (bf16[128,4096]{1,0:T(8,128)(2,1)}, bf16[128,4096]{1,0:T(8,128)(2,1)}, u32[]{:S(2)}, u32[]{:S(2)}) collective-permute-start(bf16[128,4096]{1,0:T(8,128)(2,1)} %get-tuple-element.46), channel_id=1, source_target_pairs={{0,32},{1,33},{16,48},{17,49},{32,1},{33,0},{48,17},{49,16},{64,96... | collective-permute-start | bytes 3145736 | tf_op jit(solution)/shard_map/ppermute | solution.py:157
  11.7 39.4 %collective-permute-start.2 = (bf16[128,4096]{1,0:T(8,128)(2,1)S(1)}, bf16[128,4096]{1,0:T(8,128)(2,1)}, u32[]{:S(2)}, u32[]{:S(2)}) collective-permute-start(bf16[128,4096]{1,0:T(8,128)(2,1)S(1)} %get-tuple-element.45), channel_id=1, source_target_pairs={{0,33},{1,32},{16,49},{17,48},{32,0},{33,1},{48,16},{49,17},{64,97... | collective-permute-start | bytes 3145736 | tf_op jit(solution)/shard_map/ppermute | solution.py:158
  47.3 29.3 %collective-permute-start.1 = (bf16[128,4096]{1,0:T(8,128)(2,1)}, bf16[128,4096]{1,0:T(8,128)(2,1)}, u32[]{:S(2)}, u32[]{:S(2)}) collective-permute-start(bf16[128,4096]{1,0:T(8,128)(2,1)} %collective-permute-done), channel_id=1, source_target_pairs={{0,32},{1,33},{16,48},{17,49},{32,1},{33,0},{48,17},{49,16},{64,96... | collective-permute-start | bytes 3145736 | tf_op jit(solution)/shard_map/ppermute | solution.py:159
  51.1 27.8 %collective-permute-start.3 = (bf16[128,4096]{1,0:T(8,128)(2,1)}, bf16[128,4096]{1,0:T(8,128)(2,1)S(1)}, u32[]{:S(2)}, u32[]{:S(2)}) collective-permute-start(bf16[128,4096]{1,0:T(8,128)(2,1)} %collective-permute-done.2), channel_id=1, source_target_pairs={{0,33},{1,32},{16,49},{17,48},{32,0},{33,1},{48,16},{49,17},{64,97... | collective-permute-start | bytes 3145736 | tf_op jit(solution)/shard_map/ppermute | solution.py:160
  80.0 2.9 %copy-start.3 = (bf16[8192,256]{1,0:T(8,128)(2,1)S(1)}, bf16[8192,256]{1,0:T(8,128)(2,1)}, u32[]{:S(2)}) copy-start(bf16[8192,256]{1,0:T(8,128)(2,1)} %all-gather.3.cloned.1.call-done) | copy-start | bytes 12582916
  85.3 14.5 %copy-start.4 = (bf16[256,128]{1,0:T(8,128)(2,1)}, bf16[256,128]{1,0:T(8,128)(2,1)S(1)}, u32[]{:S(2)}) copy-start(bf16[256,128]{1,0:T(8,128)(2,1)S(1)} %slice.231) | copy-start | bytes 196612
  85.6 14.2 %copy-start.6 = (bf16[256,128]{1,0:T(8,128)(2,1)}, bf16[256,128]{1,0:T(8,128)(2,1)S(1)}, u32[]{:S(2)}) copy-start(bf16[256,128]{1,0:T(8,128)(2,1)S(1)} %fusion.40) | copy-start | bytes 196612
  86.3 61.2 %collective-permute-start.5 = (bf16[272,256]{1,0:T(8,128)(2,1)}, bf16[272,256]{1,0:T(8,128)(2,1)}, u32[]{:S(2)}, u32[]{:S(2)}) collective-permute-start(bf16[272,256]{1,0:T(8,128)(2,1)} %fusion.35), channel_id=1, source_target_pairs={{0,6},{2,8},{4,10},{6,12},{8,14},{1,7},{3,9},{5,11},{7,13},{9,15},... | collective-permute-start | bytes 417800 | tf_op jit(solution)/shard_map/ppermute | solution.py:203
  93.6 54.8 %collective-permute-start.6 = (bf16[272,256]{1,0:T(8,128)(2,1)}, bf16[272,256]{1,0:T(8,128)(2,1)}, u32[]{:S(2)}, u32[]{:S(2)}) collective-permute-start(bf16[272,256]{1,0:T(8,128)(2,1)} %fusion.35), channel_id=1, source_target_pairs={{0,4},{2,6},{4,8},{6,10},{8,12},{10,14},{1,5},{3,7},{5,9},{7,11},{... | collective-permute-start | bytes 417800 | tf_op jit(solution)/shard_map/ppermute | solution.py:203
  95.6 53.8 %collective-permute-start.7 = (bf16[272,256]{1,0:T(8,128)(2,1)}, bf16[272,256]{1,0:T(8,128)(2,1)}, u32[]{:S(2)}, u32[]{:S(2)}) collective-permute-start(bf16[272,256]{1,0:T(8,128)(2,1)} %fusion.35), channel_id=1, source_target_pairs={{0,2},{2,4},{4,6},{6,8},{8,10},{10,12},{12,14},{1,3},{3,5},{5,7},{... | collective-permute-start | bytes 417800 | tf_op jit(solution)/shard_map/ppermute | solution.py:203
  104.5 3.0 %copy-start.2 = (bf16[8192,256]{1,0:T(8,128)(2,1)S(1)}, bf16[8192,256]{1,0:T(8,128)(2,1)}, u32[]{:S(2)}) copy-start(bf16[8192,256]{1,0:T(8,128)(2,1)} %all-gather.5.cloned.1.call-done) | copy-start | bytes 12582916
  109.8 40.5 %copy-start.5 = (bf16[256,128]{1,0:T(8,128)(2,1)S(1)}, bf16[256,128]{1,0:T(8,128)(2,1)}, u32[]{:S(2)}) copy-start(bf16[256,128]{1,0:T(8,128)(2,1)} %copy-done.4) | copy-start | bytes 196612
  109.9 40.5 %copy-start.7 = (bf16[256,128]{1,0:T(8,128)(2,1)S(1)}, bf16[256,128]{1,0:T(8,128)(2,1)}, u32[]{:S(2)}) copy-start(bf16[256,128]{1,0:T(8,128)(2,1)} %copy-done.6) | copy-start | bytes 196612
  110.6 20.6 %collective-permute-start.4 = (bf16[144,256]{1,0:T(8,128)(2,1)S(1)}, bf16[144,256]{1,0:T(8,128)(2,1)S(1)}, u32[]{:S(2)}, u32[]{:S(2)}) collective-permute-start(bf16[144,256]{1,0:T(8,128)(2,1)S(1)} %fusion.43), channel_id=1, source_target_pairs={{0,8},{2,10},{4,12},{6,14},{1,9},{3,11},{5,13},{7,15},{16,24},{18,... | collective-permute-start | bytes 221192 | tf_op jit(solution)/shard_map/ppermute | solution.py:203
  117.4 38.5 %copy-start = (bf16[1,256,4096]{2,1,0:T(8,128)(2,1)S(1)}, bf16[1,256,4096]{2,1,0:T(8,128)(2,1)}, u32[]{:S(2)}) copy-start(bf16[1,256,4096]{2,1,0:T(8,128)(2,1)} %param.14) | copy-start | bytes 6291460
  117.4 3.3 %collective-permute-start.8 = (bf16[128,256]{1,0:T(8,128)(2,1)S(1)}, bf16[128,256]{1,0:T(8,128)(2,1)S(1)}, u32[]{:S(2)}, u32[]{:S(2)}) collective-permute-start(bf16[128,256]{1,0:T(8,128)(2,1)S(1)} %fusion.44), channel_id=1, source_target_pairs={{0,8},{2,10},{4,12},{6,14},{1,9},{3,11},{5,13},{7,15},{16,24},{18,... | collective-permute-start | bytes 196616 | tf_op jit(solution)/shard_map/ppermute | solution.py:203
  120.7 19.5 %collective-permute-start.9 = (bf16[256,256]{1,0:T(8,128)(2,1)S(1)}, bf16[256,256]{1,0:T(8,128)(2,1)S(1)}, u32[]{:S(2)}, u32[]{:S(2)}) collective-permute-start(bf16[256,256]{1,0:T(8,128)(2,1)S(1)} %pad_maximum_fusion.3), channel_id=1, source_target_pairs={{0,6},{2,8},{4,10},{6,12},{8,14},{1,7},{3,9},{5,11},{7,13},{9,15},... | collective-permute-start | bytes 393224 | tf_op jit(solution)/shard_map/ppermute | solution.py:203
  131.2 12.0 %collective-permute-start.10 = (bf16[256,256]{1,0:T(8,128)(2,1)S(1)}, bf16[256,256]{1,0:T(8,128)(2,1)S(1)}, u32[]{:S(2)}, u32[]{:S(2)}) collective-permute-start(bf16[256,256]{1,0:T(8,128)(2,1)S(1)} %pad_maximum_fusion.3), channel_id=1, source_target_pairs={{0,4},{2,6},{4,8},{6,10},{8,12},{10,14},{1,5},{3,7},{5,9},{7,11},{... | collective-permute-start | bytes 393224 | tf_op jit(solution)/shard_map/ppermute | solution.py:203
  140.3 7.2 %collective-permute-start.11 = (bf16[256,256]{1,0:T(8,128)(2,1)S(1)}, bf16[256,256]{1,0:T(8,128)(2,1)S(1)}, u32[]{:S(2)}, u32[]{:S(2)}) collective-permute-start(bf16[256,256]{1,0:T(8,128)(2,1)S(1)} %pad_maximum_fusion.3), channel_id=1, source_target_pairs={{0,2},{2,4},{4,6},{6,8},{8,10},{10,12},{12,14},{1,3},{3,5},{5,7},{... | collective-permute-start | bytes 393224 | tf_op jit(solution)/shard_map/ppermute | solution.py:203
Sparse Core Ops, SparseCore 0:
  9.2 52.5 all-gather.2
  63.6 40.8 all-gather.4

commit v4 on v2

--- a/solution.py
+++ b/solution.py
@@ -49,7 +49,8 @@
     return vectors * cosine[:, None, :] + turned * sine_table[:, None, :]
 
 
-def dense_kernel(vis_ref, cos_ref, sin_ref, q_ref, k_ref, v_ref, o_ref, qs_ref):
+def dense_kernel(vis_ref, cos_ref, sin_ref, q_ref, k_ref, v_ref, *rest):
+    o_ref, qs_ref = rest[-2:]
     rows = o_ref.shape[0]
     group = o_ref.shape[1] // HD
     cosine = cos_ref[...]
@@ -84,7 +85,7 @@
             o_ref[:, head * HD:(head + 1) * HD] = result[g].astype(o_ref.dtype)
 
 
-def dense_attention(visible, cosine, signed_sine, query_rot, kv_all, kv_heads, head):
+def dense_attention(visible, cosine, signed_sine, query_rot, kv_all, kv_heads, head, into=None):
     row_count, width = query_rot.shape
     height = kv_all.shape[0]
     q_blocks = row_count // BLOCK
@@ -100,17 +101,19 @@
             pl.BlockSpec((BLOCK, group_width), lambda qb: (qb, head)),
             pl.BlockSpec((height, HD), lambda qb: (0, 0)),
             pl.BlockSpec((height, HD), lambda qb: (0, 1)),
-        ],
-        out_specs=pl.BlockSpec((BLOCK, group_width), lambda qb: (qb, 0)),
+        ]
+        + ([] if into is None else [pl.BlockSpec(memory_space=pl.ANY)]),
+        out_specs=pl.BlockSpec((BLOCK, group_width), lambda qb: (qb, head)),
+        input_output_aliases={} if into is None else {6: 0},
         scratch_shapes=[pltpu.VMEM((group * BLOCK, HD), jnp.bfloat16)],
-        out_shape=jax.ShapeDtypeStruct((row_count, group_width), jnp.bfloat16),
+        out_shape=jax.ShapeDtypeStruct((row_count, width), jnp.bfloat16),
         compiler_params=pltpu.CompilerParams(vmem_limit_bytes=48 * 1024 * 1024),
         cost_estimate=pl.CostEstimate(
             flops=4 * row_count * group_width * height,
             transcendentals=row_count * group * height,
             bytes_accessed=4 * row_count * group_width + 2 * kv_all.size + 4 * row_count * height,
         ),
-    )(visible, cosine, signed_sine, query_rot, kv_all, kv_all)
+    )(visible, cosine, signed_sine, query_rot, kv_all, kv_all, *([] if into is None else [into]))
 
 
 def shift_pairs(count, step):
@@ -144,7 +147,7 @@
         local_docs = doc_blocks[0]
         blocks_here = row_count // BLOCK
 
-        outputs = []
+        context = None
         visible = None
         earlier_rows = None
         for head in range(kv_heads):
@@ -204,12 +207,9 @@
                     & (key_pos[None, :] >= 0)
                     & (key_docs[None, :] == query_docs[:, None])
                 ).astype(jnp.int32)
-            outputs.append(
-                dense_attention(
-                    visible, kernel_cosine, signed_sine, query_rot, kv_all, kv_heads, head
-                )
+            context = dense_attention(
+                visible, kernel_cosine, signed_sine, query_rot, kv_all, kv_heads, head, context
             )
-        context = jnp.concatenate(outputs, axis=1)
         return context[None]
 
     return body

time: 192 us -> 192 us (level)
  no operation moved by 1% of the time
where the time goes in v4:
time: 192 us; the launch traced here: 190 us
  waiting for transfers between devices  92.2 us (48%)
  starting transfers between devices  32.6 us (17%)
  Pallas kernels  24.8 us (13%)
  between operations  15 us (8%)
  other arithmetic  10.6 us (6%)
  matrix products  7.62 us (4%)
  local copies, waits for them, and re-layouts  7.23 us (4%)
    all_gather x2, waiting for transfers between devices, layer(): weights = lax.all_gather(joined, 'dp', axis=0, tiled=True)  68.9 us
    ppermute x8, starting transfers between devices, layer(): arrived = lax.ppermute(payload, 'ctx', pairs)  32 us
    pallas_call x2, Pallas kernels, dense_attention(): pl.pallas_call(dense_kernel, grid=(q_blocks,), in_specs=[pl.BlockSpec((BL...  24.8 us
    ppermute x8, waiting for transfers between devices, layer(): arrived = lax.ppermute(payload, 'ctx', pairs)  13.6 us
    ppermute x1, waiting for transfers between devices, layer(): partner_tokens = lax.ppermute(local_tokens, 'tp', [(0, 1), (1, 0)])  9.71 us
    dot_general x2, matrix products, layer(): jnp.dot(local_tokens, weights[tp_rank], preferred_element_type=jnp.float32)  6.15 us
  transfers between devices with their start and end apart: 11, of which 7 were waited for; matrix products, arithmetic and copies ran while one was open for 9% of the time, Pallas kernels for 0%

profile of v4, /device:TPU:100, one launch (start us, length us, event | category | flops | bytes accessed | tf_op | source)
XLA Modules:
  0.0 190.1 jit_solution(10337621902893960993)
XLA Ops:
  6.5 1.2 fusion.50
  11.8 1.0 multiply_sine_fusion
  12.9 52.4 %all-gather.3.cloned.1.call-done = bf16[8192,256]{1,0:T(8,128)(2,1)} async-done(((bf16[512,256]{1,0:T(8,128)(2,1)}), bf16[8192,256]{1,0:T(8,128)(2,1)}) %all-gather.3.cloned.1.call-update) | async-done | bytes 4194320 | tf_op jit(solution)/shard_map/all_gather | solution.py:156
  65.3 3.1 %fusion.6 = f32[256,256]{0,1:T(8,128)S(1)} fusion(bf16[2,4096,256]{2,1,0:T(8,128)(2,1)} %bitcast.77, s32[]{:T(128)S(6)} %select_n.8, bf16[1,256,4096]{2,1,0:T(8,128)(2,1)} %param.13), kind=kOutput, calls=%fused_computation.6 | convolution fusion | flops 536870912 | bytes 4456452 | tf_op jit(solution)/shard_map/dot_general | solution.py:158
  68.4 9.7 %collective-permute-done = bf16[256,4096]{1,0:T(8,128)(2,1)S(1)} collective-permute-done((bf16[256,4096]{1,0:T(8,128)(2,1)}, bf16[256,4096]{1,0:T(8,128)(2,1)S(1)}, u32[]{:S(2)}, u32[]{:S(2)}) %collective-permute-start) | collective-permute-done | bytes 2097184 | tf_op jit(solution)/shard_map/ppermute | solution.py:146
  79.9 5.9 %collective-permute-start.2 = (bf16[272,256]{1,0:T(8,128)(2,1)}, bf16[272,256]{1,0:T(8,128)(2,1)}, u32[]{:S(2)}, u32[]{:S(2)}) collective-permute-start(bf16[272,256]{1,0:T(8,128)(2,1)} %fusion.29), channel_id=1, source_target_pairs={{0,6},{2,8},{4,10},{6,12},{8,14},{1,7},{3,9},{5,11},{7,13},{9,15},... | collective-permute-start | bytes 417800 | tf_op jit(solution)/shard_map/ppermute | solution.py:188
  85.8 1.9 %collective-permute-start.3 = (bf16[272,256]{1,0:T(8,128)(2,1)}, bf16[272,256]{1,0:T(8,128)(2,1)}, u32[]{:S(2)}, u32[]{:S(2)}) collective-permute-start(bf16[272,256]{1,0:T(8,128)(2,1)} %fusion.29), channel_id=1, source_target_pairs={{0,4},{2,6},{4,8},{6,10},{8,12},{10,14},{1,5},{3,7},{5,9},{7,11},{... | collective-permute-start | bytes 417800 | tf_op jit(solution)/shard_map/ppermute | solution.py:188
  87.7 2.9 %collective-permute-start.4 = (bf16[272,256]{1,0:T(8,128)(2,1)}, bf16[272,256]{1,0:T(8,128)(2,1)}, u32[]{:S(2)}, u32[]{:S(2)}) collective-permute-start(bf16[272,256]{1,0:T(8,128)(2,1)} %fusion.29), channel_id=1, source_target_pairs={{0,2},{2,4},{4,6},{6,8},{8,10},{10,12},{12,14},{1,3},{3,5},{5,7},{... | collective-permute-start | bytes 417800 | tf_op jit(solution)/shard_map/ppermute | solution.py:188
  91.3 16.5 %all-gather.5.cloned.1.call-done = bf16[8192,256]{1,0:T(8,128)(2,1)} async-done(((bf16[512,256]{1,0:T(8,128)(2,1)}), bf16[8192,256]{1,0:T(8,128)(2,1)}) %all-gather.5.cloned.1.call-update) | async-done | bytes 4194320 | tf_op jit(solution)/shard_map/all_gather | solution.py:156
  107.7 3.1 %fusion.2 = f32[256,256]{0,1:T(8,128)S(1)} fusion(bf16[2,4096,256]{2,1,0:T(8,128)(2,1)} %bitcast.75, s32[]{:T(128)S(6)} %select_n.8, bf16[1,256,4096]{2,1,0:T(8,128)(2,1)} %param.13), kind=kOutput, calls=%fused_computation.2 | convolution fusion | flops 536870912 | bytes 4456452 | tf_op jit(solution)/shard_map/dot_general | solution.py:158
  112.9 5.0 %collective-permute-start.1 = (bf16[144,256]{1,0:T(8,128)(2,1)S(1)}, bf16[144,256]{1,0:T(8,128)(2,1)S(1)}, u32[]{:S(2)}, u32[]{:S(2)}) collective-permute-start(bf16[144,256]{1,0:T(8,128)(2,1)S(1)} %fusion.37), channel_id=1, source_target_pairs={{0,8},{2,10},{4,12},{6,14},{1,9},{3,11},{5,13},{7,15},{16,24},{18,... | collective-permute-start | bytes 221192 | tf_op jit(solution)/shard_map/ppermute | solution.py:188
  118.2 1.4 collective-permute-start.5
  119.7 1.9 collective-permute-done.5
  121.5 10.8 %collective-permute-start.6 = (bf16[256,256]{1,0:T(8,128)(2,1)S(1)}, bf16[256,256]{1,0:T(8,128)(2,1)S(1)}, u32[]{:S(2)}, u32[]{:S(2)}) collective-permute-start(bf16[256,256]{1,0:T(8,128)(2,1)S(1)} %pad_maximum_fusion.3), channel_id=1, source_target_pairs={{0,6},{2,8},{4,10},{6,12},{8,14},{1,7},{3,9},{5,11},{7,13},{9,15},... | collective-permute-start | bytes 393224 | tf_op jit(solution)/shard_map/ppermute | solution.py:188
  132.3 1.9 %collective-permute-start.7 = (bf16[256,256]{1,0:T(8,128)(2,1)S(1)}, bf16[256,256]{1,0:T(8,128)(2,1)S(1)}, u32[]{:S(2)}, u32[]{:S(2)}) collective-permute-start(bf16[256,256]{1,0:T(8,128)(2,1)S(1)} %pad_maximum_fusion.3), channel_id=1, source_target_pairs={{0,4},{2,6},{4,8},{6,10},{8,12},{10,14},{1,5},{3,7},{5,9},{7,11},{... | collective-permute-start | bytes 393224 | tf_op jit(solution)/shard_map/ppermute | solution.py:188
  135.5 6.6 %collective-permute-done.6 = bf16[256,256]{1,0:T(8,128)(2,1)S(1)} collective-permute-done((bf16[256,256]{1,0:T(8,128)(2,1)S(1)}, bf16[256,256]{1,0:T(8,128)(2,1)S(1)}, u32[]{:S(2)}, u32[]{:S(2)}) %collective-permute-start.6) | collective-permute-done | bytes 131104 | tf_op jit(solution)/shard_map/ppermute | solution.py:188
  142.1 2.1 %collective-permute-start.8 = (bf16[256,256]{1,0:T(8,128)(2,1)S(1)}, bf16[256,256]{1,0:T(8,128)(2,1)S(1)}, u32[]{:S(2)}, u32[]{:S(2)}) collective-permute-start(bf16[256,256]{1,0:T(8,128)(2,1)S(1)} %pad_maximum_fusion.3), channel_id=1, source_target_pairs={{0,2},{2,4},{4,6},{6,8},{8,10},{10,12},{12,14},{1,3},{3,5},{5,7},{... | collective-permute-start | bytes 393224 | tf_op jit(solution)/shard_map/ppermute | solution.py:188
  144.9 4.4 %collective-permute-done.8 = bf16[256,256]{1,0:T(8,128)(2,1)S(1)} collective-permute-done((bf16[256,256]{1,0:T(8,128)(2,1)S(1)}, bf16[256,256]{1,0:T(8,128)(2,1)S(1)}, u32[]{:S(2)}, u32[]{:S(2)}) %collective-permute-start.8) | collective-permute-done | bytes 131104 | tf_op jit(solution)/shard_map/ppermute | solution.py:188
  149.3 1.2 fusion.46
  150.6 1.2 fusion.45
  151.8 1.2 fusion.44
  157.5 1.0 and_convert_fusion.vis_ref
  158.5 12.4 %shard_map.55.rest_0_ = bf16[256,4096]{1,0:T(8,128)(2,1)} custom-call(s32[256,1152]{1,0:T(8,128)S(1)} %and_convert_fusion.vis_ref, f32[256,128]{1,0:T(8,128)S(1)} %get-tuple-element.61.cos_ref, f32[256,128]{1,0:T(8,128)S(1)} %get-tuple-element.62.sin_ref, bf16[256,4096]{1,0:T(8,128)(2,1)S(1)} %bitcast.72, bf16[1152,256]{1,0:T(8,128)(2,1)S(1)} %fusion.30.k_ref.v_ref, ...), custom_call_target="tpu_custom_call" | custom-call | flops 2415919104 | bytes 3866624 | tf_op jit(solution)/shard_map/pallas_call | solution.py:94
  170.9 12.4 %shard_map.56 = bf16[256,4096]{1,0:T(8,128)(2,1)} custom-call(s32[256,1152]{1,0:T(8,128)S(1)} %and_convert_fusion.vis_ref, f32[256,128]{1,0:T(8,128)S(1)} %get-tuple-element.61.cos_ref, f32[256,128]{1,0:T(8,128)S(1)} %get-tuple-element.62.sin_ref, bf16[256,4096]{1,0:T(8,128)(2,1)S(1)} %bitcast.73, ...), custom_call_target="tpu_custom_call", output_to_operand_aliasing={{}: (6, {})} | custom-call | flops 2415919104 | bytes 3866624 | tf_op jit(solution)/shard_map/pallas_call | solution.py:94
  (65 shorter events, 14.0 us)
Async XLA Ops:
  6.5 6.2 %copy-start.5 = (f32[128]{0:T(128)S(1)}, f32[128]{0:T(128)}, u32[]{:S(2)}) copy-start(f32[128]{0:T(128)} %constant.128.clone.1) | copy-start | bytes 1540
  6.5 3.3 %copy-start.6 = (s32[1,2]{1,0:T(1,128)S(1)}, s32[1,2]{1,0:T(1,128)}, u32[]{:S(2)}) copy-start(s32[1,2]{1,0:T(1,128)} %param.17) | copy-start | bytes 28
  6.5 58.8 %all-gather.3.cloned.1.call-start = ((), (), s32[]{:S(2)}) async-start(), calls=%async_computation | async-start | bytes 4456448 | tf_op jit(solution)/shard_map/all_gather | solution.py:156
  8.5 99.3 %all-gather.5.cloned.1.call-start = ((), (), s32[]{:S(2)}) async-start(), calls=%async_computation.1 | async-start | bytes 4456448 | tf_op jit(solution)/shard_map/all_gather | solution.py:156
  9.3 68.8 %collective-permute-start = (bf16[256,4096]{1,0:T(8,128)(2,1)}, bf16[256,4096]{1,0:T(8,128)(2,1)S(1)}, u32[]{:S(2)}, u32[]{:S(2)}) collective-permute-start(bf16[256,4096]{1,0:T(8,128)(2,1)} %bitcast.74), channel_id=1, source_target_pairs={{0,1},{1,0},{2,3},{3,2},{4,5},{5,4},{6,7},{7,6},{8,9},{9,8},{10,11... | collective-permute-start | bytes 6291464 | tf_op jit(solution)/shard_map/ppermute | solution.py:146
  65.3 12.8 %copy-start.2 = (bf16[8192,256]{1,0:T(8,128)(2,1)S(1)}, bf16[8192,256]{1,0:T(8,128)(2,1)}, u32[]{:S(2)}) copy-start(bf16[8192,256]{1,0:T(8,128)(2,1)} %all-gather.3.cloned.1.call-done) | copy-start | bytes 12582916
  78.9 12.4 %copy-start.3 = (bf16[256,128]{1,0:T(8,128)(2,1)}, bf16[256,128]{1,0:T(8,128)(2,1)S(1)}, u32[]{:S(2)}) copy-start(bf16[256,128]{1,0:T(8,128)(2,1)S(1)} %slice.213) | copy-start | bytes 196612
  79.2 12.1 %copy-start.4 = (bf16[256,128]{1,0:T(8,128)(2,1)}, bf16[256,128]{1,0:T(8,128)(2,1)S(1)}, u32[]{:S(2)}) copy-start(bf16[256,128]{1,0:T(8,128)(2,1)S(1)} %fusion.34) | copy-start | bytes 196612
  79.9 69.5 %collective-permute-start.2 = (bf16[272,256]{1,0:T(8,128)(2,1)}, bf16[272,256]{1,0:T(8,128)(2,1)}, u32[]{:S(2)}, u32[]{:S(2)}) collective-permute-start(bf16[272,256]{1,0:T(8,128)(2,1)} %fusion.29), channel_id=1, source_target_pairs={{0,6},{2,8},{4,10},{6,12},{8,14},{1,7},{3,9},{5,11},{7,13},{9,15},... | collective-permute-start | bytes 417800 | tf_op jit(solution)/shard_map/ppermute | solution.py:188
  85.8 64.8 %collective-permute-start.3 = (bf16[272,256]{1,0:T(8,128)(2,1)}, bf16[272,256]{1,0:T(8,128)(2,1)}, u32[]{:S(2)}, u32[]{:S(2)}) collective-permute-start(bf16[272,256]{1,0:T(8,128)(2,1)} %fusion.29), channel_id=1, source_target_pairs={{0,4},{2,6},{4,8},{6,10},{8,12},{10,14},{1,5},{3,7},{5,9},{7,11},{... | collective-permute-start | bytes 417800 | tf_op jit(solution)/shard_map/ppermute | solution.py:188
  87.7 64.1 %collective-permute-start.4 = (bf16[272,256]{1,0:T(8,128)(2,1)}, bf16[272,256]{1,0:T(8,128)(2,1)}, u32[]{:S(2)}, u32[]{:S(2)}) collective-permute-start(bf16[272,256]{1,0:T(8,128)(2,1)} %fusion.29), channel_id=1, source_target_pairs={{0,2},{2,4},{4,6},{6,8},{8,10},{10,12},{12,14},{1,3},{3,5},{5,7},{... | collective-permute-start | bytes 417800 | tf_op jit(solution)/shard_map/ppermute | solution.py:188
  107.7 3.7 %copy-start.1 = (bf16[8192,256]{1,0:T(8,128)(2,1)S(1)}, bf16[8192,256]{1,0:T(8,128)(2,1)}, u32[]{:S(2)}) copy-start(bf16[8192,256]{1,0:T(8,128)(2,1)} %all-gather.5.cloned.1.call-done) | copy-start | bytes 12582916
  112.9 19.4 %collective-permute-start.1 = (bf16[144,256]{1,0:T(8,128)(2,1)S(1)}, bf16[144,256]{1,0:T(8,128)(2,1)S(1)}, u32[]{:S(2)}, u32[]{:S(2)}) collective-permute-start(bf16[144,256]{1,0:T(8,128)(2,1)S(1)} %fusion.37), channel_id=1, source_target_pairs={{0,8},{2,10},{4,12},{6,14},{1,9},{3,11},{5,13},{7,15},{16,24},{18,... | collective-permute-start | bytes 221192 | tf_op jit(solution)/shard_map/ppermute | solution.py:188
  118.2 40.3 %copy-start = (bf16[1,256,4096]{2,1,0:T(8,128)(2,1)S(1)}, bf16[1,256,4096]{2,1,0:T(8,128)(2,1)}, u32[]{:S(2)}) copy-start(bf16[1,256,4096]{2,1,0:T(8,128)(2,1)} %param.14) | copy-start | bytes 6291460
  118.2 3.3 %collective-permute-start.5 = (bf16[128,256]{1,0:T(8,128)(2,1)S(1)}, bf16[128,256]{1,0:T(8,128)(2,1)S(1)}, u32[]{:S(2)}, u32[]{:S(2)}) collective-permute-start(bf16[128,256]{1,0:T(8,128)(2,1)S(1)} %fusion.38), channel_id=1, source_target_pairs={{0,8},{2,10},{4,12},{6,14},{1,9},{3,11},{5,13},{7,15},{16,24},{18,... | collective-permute-start | bytes 196616 | tf_op jit(solution)/shard_map/ppermute | solution.py:188
  121.5 20.5 %collective-permute-start.6 = (bf16[256,256]{1,0:T(8,128)(2,1)S(1)}, bf16[256,256]{1,0:T(8,128)(2,1)S(1)}, u32[]{:S(2)}, u32[]{:S(2)}) collective-permute-start(bf16[256,256]{1,0:T(8,128)(2,1)S(1)} %pad_maximum_fusion.3), channel_id=1, source_target_pairs={{0,6},{2,8},{4,10},{6,12},{8,14},{1,7},{3,9},{5,11},{7,13},{9,15},... | collective-permute-start | bytes 393224 | tf_op jit(solution)/shard_map/ppermute | solution.py:188
  132.3 12.6 %collective-permute-start.7 = (bf16[256,256]{1,0:T(8,128)(2,1)S(1)}, bf16[256,256]{1,0:T(8,128)(2,1)S(1)}, u32[]{:S(2)}, u32[]{:S(2)}) collective-permute-start(bf16[256,256]{1,0:T(8,128)(2,1)S(1)} %pad_maximum_fusion.3), channel_id=1, source_target_pairs={{0,4},{2,6},{4,8},{6,10},{8,12},{10,14},{1,5},{3,7},{5,9},{7,11},{... | collective-permute-start | bytes 393224 | tf_op jit(solution)/shard_map/ppermute | solution.py:188
  142.1 7.2 %collective-permute-start.8 = (bf16[256,256]{1,0:T(8,128)(2,1)S(1)}, bf16[256,256]{1,0:T(8,128)(2,1)S(1)}, u32[]{:S(2)}, u32[]{:S(2)}) collective-permute-start(bf16[256,256]{1,0:T(8,128)(2,1)S(1)} %pad_maximum_fusion.3), channel_id=1, source_target_pairs={{0,2},{2,4},{4,6},{6,8},{8,10},{10,12},{12,14},{1,3},{3,5},{5,7},{... | collective-permute-start | bytes 393224 | tf_op jit(solution)/shard_map/ppermute | solution.py:188
Sparse Core Ops, SparseCore 0:
  9.2 56.0 all-gather.2
  67.2 40.5 all-gather.4
